TPU v7x, 512 devices: a whole 4x8x8 slice. The times are simulated.
512 devices in a mesh: ctx: 64 (over y_hi, x, z), head: 8 (over y_lo, core).
Axes of the slice: x: 4, y: 8 (y_hi: 2, y_lo: 4; y = y_hi * 4 + y_lo), z: 8, core: 2. Of those that a mesh axis runs over, the one named last changes fastest.
Arguments:
- q_self: bfloat16 [8192, 4096], P('ctx', 'head'), may hold values from -6 to 6
- k_self: bfloat16 [8192, 4096], P('ctx', 'head'), may hold values from -6 to 6
- v_self: bfloat16 [8192, 4096], P('ctx', 'head'), may hold values from -6 to 6
- q_cross: bfloat16 [8192, 4096], P('ctx', 'head'), may hold values from -6 to 6
- n_keys: bfloat16 [32768, 4096], P('ctx', 'head'), may hold values from -6 to 6
- n_values: bfloat16 [32768, 4096], P('ctx', 'head'), may hold values from -6 to 6
- d_cross: bfloat16 [8192, 4096], P('ctx', 'head'), may hold values from -16 to 16
Outputs:
- self_out: bfloat16 [8192, 4096], P('ctx', 'head')
- cross_out: bfloat16 [8192, 4096], P('ctx', 'head')
- d_query: bfloat16 [8192, 4096], P('ctx', 'head')
- d_keys: bfloat16 [32768, 4096], P('ctx', 'head')
- d_values: bfloat16 [32768, 4096], P('ctx', 'head')
All inputs are finite; a program needn't handle non-finite values.
Results may differ from a plain program's by a relative error of at most 0.012.
Values may be sent and summed in bfloat16 or wider, within the bound.
No kernel may reach another device: no remote copies, remote signals or barrier semaphores. Data moves between devices by JAX's collectives and lax.ppermute only.
A program may use at most 128 MiB of HBM per device.

v0:
```python
import math

import jax
import jax.numpy as jnp
from jax import lax
from jax.sharding import PartitionSpec as P

HD = 128
SPAN = 64


def from_behind(block, axis, distance):
    devices = range(lax.axis_size(axis))
    route = [(i - distance, i) for i in devices if i - distance in devices]
    return lax.ppermute(block, axis, route)


def attend_block(folded, keys_block, values_block, key_first, queries, positions):
    running_max, running_sum, accumulated = folded
    scores = jnp.einsum("rhd,khd->hrk", queries, keys_block, preferred_element_type=jnp.float32) * (
        1.0 / math.sqrt(HD)
    )
    key_positions = key_first + jnp.arange(keys_block.shape[0], dtype=jnp.int32)
    visible = (key_positions[None, :] <= positions[:, None])[None]
    masked = jnp.where(visible, scores, jnp.float32(-1e30))
    new_max = jnp.maximum(running_max, jnp.max(masked, axis=2))
    weights = jnp.where(visible, jnp.exp(masked - new_max[:, :, None]), jnp.float32(0.0))
    rescale = jnp.exp(running_max - new_max)
    new_sum = running_sum * rescale + jnp.sum(weights, axis=2)
    product = jnp.einsum(
        "hrk,khd->hrd",
        weights.astype(jnp.bfloat16),
        values_block,
        preferred_element_type=jnp.float32,
    )
    return (new_max, new_sum, accumulated * rescale[:, :, None] + product)


def self_attention(groups, keys_local, values_local):
    column_count = keys_local.shape[1]
    head_count = column_count // HD
    prepared = []
    for queries_flat, positions in groups:
        row_count = queries_flat.shape[0]
        prepared.append(
            (queries_flat.reshape(row_count, head_count, HD), positions, jnp.max(positions))
        )
    initial = tuple(
        (
            (
                jnp.full((head_count, entry[0].shape[0]), -1e30, jnp.float32),
                jnp.zeros((head_count, entry[0].shape[0]), jnp.float32),
                jnp.zeros((head_count, entry[0].shape[0], HD), jnp.float32),
            )
            for entry in prepared
        )
    )
    folded = initial
    keys_piece = lax.all_gather(keys_local, "ctx", axis=0, tiled=True)
    values_piece = lax.all_gather(values_local, "ctx", axis=0, tiled=True)
    piece_rows = keys_piece.shape[0]
    block_rows = 512
    block_count = piece_rows // block_rows
    key_blocks = keys_piece.reshape(block_count, block_rows, head_count, HD)
    value_blocks = values_piece.reshape(block_count, block_rows, head_count, HD)

    def visit(inner, items):
        keys_block, values_block, block_index = items
        key_first = block_index * block_rows
        updated = []
        for state, entry in zip(inner, prepared):
            queries, positions, last_position = entry

            def update(current, queries=queries, positions=positions):
                return attend_block(
                    current, keys_block, values_block, key_first, queries, positions
                )

            def unchanged(current):
                return current

            updated.append(lax.cond(key_first <= last_position, update, unchanged, state))
        return (tuple(updated), None)

    folded, unused = lax.scan(
        visit, folded, (key_blocks, value_blocks, jnp.arange(block_count, dtype=jnp.int32))
    )
    outputs = []
    for state in folded:
        running_max, running_sum, accumulated = state
        mixed = accumulated / running_sum[:, :, None]
        row_count = mixed.shape[1]
        outputs.append(
            mixed.transpose(1, 0, 2).reshape(row_count, column_count).astype(jnp.bfloat16)
        )
    return outputs


def cross_attention(q_cross, n_keys, n_values, d_cross):
    row_count, column_count = q_cross.shape
    head_count = column_count // HD
    lag_rows = SPAN - 1
    scale_factor = 1.0 / math.sqrt(HD)
    incoming = from_behind(q_cross[:lag_rows], "ctx", -1)
    shifted = jnp.concatenate([q_cross[lag_rows:], incoming], axis=0)
    span_count = row_count // SPAN
    neighbour_rows = n_keys.shape[0] // span_count
    queries = shifted.reshape(span_count, SPAN, head_count, HD)
    neighbour_keys = n_keys.reshape(span_count, neighbour_rows, head_count, HD)
    neighbour_values = n_values.reshape(span_count, neighbour_rows, head_count, HD)
    grad_rows = d_cross.reshape(span_count, SPAN, head_count, HD)
    scores = (
        jnp.einsum("crhd,ckhd->chrk", queries, neighbour_keys, preferred_element_type=jnp.float32)
        * scale_factor
    )
    row_max = jnp.max(scores, axis=3, keepdims=True)
    weights = jnp.exp(scores - row_max)
    probs = weights / jnp.sum(weights, axis=3, keepdims=True)
    probs_low = probs.astype(jnp.bfloat16)
    attended = jnp.einsum(
        "chrk,ckhd->crhd", probs_low, neighbour_values, preferred_element_type=jnp.float32
    )
    cross_out = attended.reshape(row_count, column_count).astype(jnp.bfloat16)
    grad_probs = jnp.einsum(
        "crhd,ckhd->chrk", grad_rows, neighbour_values, preferred_element_type=jnp.float32
    )
    centre = jnp.sum(grad_probs * probs, axis=3, keepdims=True)
    grad_scores = (probs * (grad_probs - centre) * scale_factor).astype(jnp.bfloat16)
    grad_source = jnp.einsum(
        "chrk,ckhd->crhd", grad_scores, neighbour_keys, preferred_element_type=jnp.float32
    )
    grad_source = grad_source.reshape(row_count, column_count).astype(jnp.bfloat16)
    grad_keys = jnp.einsum(
        "chrk,crhd->ckhd", grad_scores, queries, preferred_element_type=jnp.float32
    ).reshape(n_keys.shape)
    grad_values = jnp.einsum(
        "chrk,crhd->ckhd", probs_low, grad_rows, preferred_element_type=jnp.float32
    ).reshape(n_values.shape)
    carried = from_behind(grad_source[row_count - lag_rows :], "ctx", 1)
    d_query = jnp.concatenate([carried, grad_source[: row_count - lag_rows]], axis=0)
    squares = jnp.sum(grad_keys * grad_keys) + jnp.sum(grad_values * grad_values)
    overall = lax.psum(squares, ("ctx", "head"))
    element_count = 2.0 * grad_keys.size * lax.axis_size("ctx") * lax.axis_size("head")
    factor = lax.rsqrt(overall / element_count + 1e-06)
    d_keys = (grad_keys * factor).astype(jnp.bfloat16)
    d_values = (grad_values * factor).astype(jnp.bfloat16)
    return (cross_out, d_query, d_keys, d_values)


def body(q_self, k_self, v_self, q_cross, n_keys, n_values, d_cross):
    row_count = q_self.shape[0]
    device_index = lax.axis_index("ctx")
    first_row = device_index * row_count
    own_positions = first_row + jnp.arange(row_count, dtype=jnp.int32)
    self_out = self_attention([(q_self, own_positions)], k_self, v_self)[0]
    cross_out, d_query, d_keys, d_values = cross_attention(q_cross, n_keys, n_values, d_cross)
    return (self_out, cross_out, d_query, d_keys, d_values)


def solution(mesh):
    in_specs = (
        P("ctx", "head"),
        P("ctx", "head"),
        P("ctx", "head"),
        P("ctx", "head"),
        P("ctx", "head"),
        P("ctx", "head"),
        P("ctx", "head"),
    )
    out_specs = (
        P("ctx", "head"),
        P("ctx", "head"),
        P("ctx", "head"),
        P("ctx", "head"),
        P("ctx", "head"),
    )
    return jax.shard_map(body, mesh=mesh, in_specs=in_specs, out_specs=out_specs, check_vma=False)
```

profile of v0, /device:TPU:54, one launch (start us, length us, event | category | flops | bytes accessed | tf_op | source)
XLA Modules:
  0.0 502.9 jit_solution(6560523842506963549)
XLA Ops:
  9.5 11.2 %collective-permute-start = (bf16[63,512]{1,0:T(8,128)(2,1)S(1)}, bf16[63,512]{1,0:T(8,128)(2,1)S(1)}, u32[]{:S(2)}, u32[]{:S(2)}) collective-permute-start(bf16[63,512]{1,0:T(8,128)(2,1)S(1)} %slice.13), channel_id=1, source_target_pairs={{8,0},{16,8},{24,16},{32,24},{40,32},{48,40},{56,48},{64,56},{72,6... | collective-permute-start | bytes 193544 | tf_op jit(solution)/shard_map/ppermute | solution.py:15
  34.1 4.7 multiply_reduce_fusion.1
  41.9 143.9 %psum.7 = f32[]{:T(128)} all-reduce(f32[]{:T(128)S(6)} %add.41), channel_id=1, replica_groups=mesh['ctx'=64,'head'=8] {'ctx','head'}, use_global_device_ids=true, to_apply=%region_12.13 | all-reduce | flops 1 | bytes 8 | tf_op jit(solution)/shard_map/psum | solution.py:142
  191.8 12.7 %all-gather.3.cloned.1.call-done = bf16[8192,512]{1,0:T(8,128)(2,1)} async-done(((bf16[128,512]{1,0:T(8,128)(2,1)}), bf16[8192,512]{1,0:T(8,128)(2,1)}) %all-gather.3.cloned.1.call-update) | async-done | bytes 8388624 | tf_op jit(solution)/shard_map/all_gather | solution.py:59
  204.5 12.5 %reshape.91 = bf16[16,512,4,128]{3,2,1,0:T(4,128)(2,1)} reshape(bf16[8192,512]{1,0:T(8,128)(2,1)} %all-gather.3.cloned.1.call-done) | data formatting | bytes 16777216 | tf_op jit(solution)/shard_map/reshape | solution.py:64
  217.1 8.9 %copy.24 = bf16[16,512,4,128]{3,1,2,0:T(8,128)(2,1)} copy(bf16[16,512,4,128]{3,2,1,0:T(4,128)(2,1)} %reshape.91) | data formatting | bytes 16777216
  226.0 166.7 %all-gather.5.cloned.1.call-done = bf16[8192,512]{1,0:T(8,128)(2,1)} async-done(((bf16[128,512]{1,0:T(8,128)(2,1)}), bf16[8192,512]{1,0:T(8,128)(2,1)}) %all-gather.5.cloned.1.call-update) | async-done | bytes 8388624 | tf_op jit(solution)/shard_map/all_gather | solution.py:60
  392.7 12.5 %reshape.92 = bf16[16,512,4,128]{3,2,1,0:T(4,128)(2,1)} reshape(bf16[8192,512]{1,0:T(8,128)(2,1)} %all-gather.5.cloned.1.call-done) | data formatting | bytes 16777216 | tf_op jit(solution)/shard_map/reshape | solution.py:65
  405.2 8.9 %copy.26 = bf16[16,512,4,128]{3,1,2,0:T(8,128)(2,1)} copy(bf16[16,512,4,128]{3,2,1,0:T(4,128)(2,1)} %reshape.92) | data formatting | bytes 16777216
  414.1 81.2 %while.15 = (s32[]{:T(128)}, f32[4,128]{1,0:T(4,128)S(1)}, f32[4,128]{1,0:T(4,128)S(1)}, f32[4,128,128]{2,1,0:T(8,128)S(1)}, s32[16]{0:T(128)S(1)}, /*index=5*/s...) while((s32[]{:T(128)}, f32[4,128]{1,0:T(4,128)S(1)}, ...), condition=%wide.region_6.7_spmd.clone, body=%wide.region_1.6_spmd.clone.sunk | while | flops 136775296 | bytes 5152051 | solution.py:85
  416.0 3.3 conditional.3
  426.6 3.3 conditional.3
  431.9 3.3 conditional.3
  437.2 3.3 conditional.3
  442.4 3.3 conditional.3
  447.7 3.3 conditional.3
  453.0 3.3 conditional.3
  458.3 3.3 conditional.3
  463.6 3.3 conditional.3
  468.8 3.3 conditional.3
  474.1 3.3 conditional.3
  479.4 3.3 conditional.3
  484.7 3.3 conditional.3
  490.0 3.3 conditional.3
  (215 shorter events, 86.6 us)
Async XLA Ops:
  7.2 197.4 %all-gather.3.cloned.1.call-start = ((), (), s32[]{:S(2)}) async-start(), calls=%async_computation | async-start | bytes 8519680 | tf_op jit(solution)/shard_map/all_gather | solution.py:59
  7.9 384.8 %all-gather.5.cloned.1.call-start = ((), (), s32[]{:S(2)}) async-start(), calls=%async_computation.1 | async-start | bytes 8519680 | tf_op jit(solution)/shard_map/all_gather | solution.py:60
  9.5 17.6 %collective-permute-start = (bf16[63,512]{1,0:T(8,128)(2,1)S(1)}, bf16[63,512]{1,0:T(8,128)(2,1)S(1)}, u32[]{:S(2)}, u32[]{:S(2)}) collective-permute-start(bf16[63,512]{1,0:T(8,128)(2,1)S(1)} %slice.13), channel_id=1, source_target_pairs={{8,0},{16,8},{24,16},{32,24},{40,32},{48,40},{56,48},{64,56},{72,6... | collective-permute-start | bytes 193544 | tf_op jit(solution)/shard_map/ppermute | solution.py:15
  23.1 8.4 %copy-start.1 = (f32[2,4,64,256]{3,2,1,0:T(8,128)}, f32[2,4,64,256]{3,2,1,0:T(8,128)S(1)}, u32[]{:S(2)}) copy-start(f32[2,4,64,256]{3,2,1,0:T(8,128)S(1)} %fusion.34) | copy-start | bytes 1572868
  27.2 4.4 copy-start
  28.9 3.3 copy-start.2
  40.0 150.3 %collective-permute-start.1 = (bf16[63,512]{1,0:T(8,128)(2,1)}, bf16[63,512]{1,0:T(8,128)(2,1)}, u32[]{:S(2)}, u32[]{:S(2)}) collective-permute-start(bf16[63,512]{1,0:T(8,128)(2,1)} %slice.16), channel_id=1, source_target_pairs={{0,8},{8,16},{16,24},{24,32},{32,40},{40,48},{48,56},{56,64},{64,7... | collective-permute-start | bytes 193544 | tf_op jit(solution)/shard_map/ppermute | solution.py:15
Sparse Core Ops, SparseCore 0:
  12.5 192.0 all-gather.2
  209.1 183.5 all-gather.4
where the time goes:
time: 506 us; the launch traced here: 503 us
  waiting for transfers between devices  181 us (36%)
  blocking collectives  144 us (28%)
  local copies, waits for them, and re-layouts  63.2 us (12%)
  matrix products  54 us (11%)
  loops' own time  21.4 us (4%)
  between operations  16.1 us (3%)
  starting transfers between devices  13.2 us (3%)
  other arithmetic  10.2 us (2%)
    all_gather x1, waiting for transfers between devices, self_attention(): values_piece = lax.all_gather(values_local, 'ctx', axis=0, tiled=True)  167 us
    psum x1, blocking collectives, cross_attention(): overall = lax.psum(squares, ('ctx', 'head'))  144 us
    dot_general x15, matrix products, attend_block(): jnp.einsum('hrk,khd->hrd', weights.astype(jnp.bfloat16), values_block, pr...  22.8 us
    dot_general x15, matrix products, attend_block(): jnp.einsum('rhd,khd->hrk', queries, keys_block, preferred_element_type=jn...  20.6 us
    another operation x1, loops' own time, self_attention(): lax.scan(visit, folded, (key_blocks, value_blocks, jnp.arange(block_count...  20.6 us
    unnamed x12, local copies, waits for them, and re-layouts  19.6 us
    ppermute x2, starting transfers between devices, from_behind(): return lax.ppermute(block, axis, route)  13.1 us
    all_gather x1, waiting for transfers between devices, self_attention(): keys_piece = lax.all_gather(keys_local, 'ctx', axis=0, tiled=True)  12.7 us
  transfers between devices with their start and end apart: 4, of which 2 were waited for; matrix products, arithmetic and copies ran while one was open for 9% of the time, Pallas kernels for 0%

commit v1 on v0

v1 whole, which is shorter than its diff:
```python
import math

import jax
import jax.numpy as jnp
from jax import lax
from jax.sharding import Mesh
from jax.sharding import PartitionSpec as P

HD = 128
SPAN = 64
CTX = ("outer", "z")


def from_behind(block, count, distance):
    route = [(i - distance, i) for i in range(count) if 0 <= i - distance < count]
    return lax.ppermute(block, CTX, route)


def spread(block, axis, count):
    copies = jnp.broadcast_to(block[None], (count,) + block.shape)
    return lax.all_to_all(copies, axis, 0, 0, tiled=True)


def self_attention(q_self, k_self, v_self, outer_count, z_count):
    row_count, column_count = q_self.shape
    head_count = column_count // HD
    outer_index = lax.axis_index("outer")
    z_index = lax.axis_index("z")
    pair = jnp.concatenate([k_self, v_self], axis=1)
    group = spread(pair, "z", z_count).reshape(z_count * row_count, 2 * column_count)
    keys = group[:, :column_count].reshape(z_count * row_count, head_count, HD)
    values = group[:, column_count:].reshape(z_count * row_count, head_count, HD)
    queries = spread(q_self, "outer", outer_count).reshape(outer_count, row_count, head_count, HD)
    key_first = outer_index * z_count * row_count
    key_positions = key_first + jnp.arange(z_count * row_count, dtype=jnp.int32)
    query_starts = (jnp.arange(outer_count, dtype=jnp.int32) * z_count + z_index) * row_count
    query_positions = query_starts[:, None] + jnp.arange(row_count, dtype=jnp.int32)[None, :]
    visible = (key_positions[None, None, :] <= query_positions[:, :, None])[None]
    scores = jnp.einsum("grhd,khd->hgrk", queries, keys, preferred_element_type=jnp.float32) * (
        1.0 / math.sqrt(HD)
    )
    masked = jnp.where(visible, scores, jnp.float32(-1e30))
    part_max = jnp.max(masked, axis=3)
    weights = jnp.where(visible, jnp.exp(masked - part_max[..., None]), jnp.float32(0.0))
    part_sum = jnp.sum(weights, axis=3)
    part_acc = jnp.einsum(
        "hgrk,khd->grhd", weights.astype(jnp.bfloat16), values, preferred_element_type=jnp.float32
    ).reshape(outer_count, row_count, column_count)
    stats = jnp.concatenate(
        [part_max.transpose(1, 2, 0), part_sum.transpose(1, 2, 0)], axis=2
    )
    packed = jnp.concatenate([part_acc, stats], axis=2)
    back = lax.all_to_all(packed, "outer", 0, 0, tiled=True)
    got_acc = back[:, :, :column_count].reshape(outer_count, row_count, head_count, HD)
    got_max = back[:, :, column_count : column_count + head_count]
    got_sum = back[:, :, column_count + head_count :]
    top = jnp.max(got_max, axis=0)
    rescale = jnp.exp(got_max - top[None])
    total = jnp.sum(got_sum * rescale, axis=0)
    mixed = jnp.sum(got_acc * rescale[..., None], axis=0)
    out = mixed / total[..., None]
    return out.reshape(row_count, column_count).astype(jnp.bfloat16)


def cross_attention(q_cross, n_keys, n_values, d_cross, ctx_count, element_total):
    row_count, column_count = q_cross.shape
    head_count = column_count // HD
    lag_rows = SPAN - 1
    scale_factor = 1.0 / math.sqrt(HD)
    incoming = from_behind(q_cross[:lag_rows], ctx_count, -1)
    shifted = jnp.concatenate([q_cross[lag_rows:], incoming], axis=0)
    span_count = row_count // SPAN
    neighbour_rows = n_keys.shape[0] // span_count
    queries = shifted.reshape(span_count, SPAN, head_count, HD)
    neighbour_keys = n_keys.reshape(span_count, neighbour_rows, head_count, HD)
    neighbour_values = n_values.reshape(span_count, neighbour_rows, head_count, HD)
    grad_rows = d_cross.reshape(span_count, SPAN, head_count, HD)
    scores = (
        jnp.einsum("crhd,ckhd->chrk", queries, neighbour_keys, preferred_element_type=jnp.float32)
        * scale_factor
    )
    row_max = jnp.max(scores, axis=3, keepdims=True)
    weights = jnp.exp(scores - row_max)
    probs = weights / jnp.sum(weights, axis=3, keepdims=True)
    probs_low = probs.astype(jnp.bfloat16)
    attended = jnp.einsum(
        "chrk,ckhd->crhd", probs_low, neighbour_values, preferred_element_type=jnp.float32
    )
    cross_out = attended.reshape(row_count, column_count).astype(jnp.bfloat16)
    grad_probs = jnp.einsum(
        "crhd,ckhd->chrk", grad_rows, neighbour_values, preferred_element_type=jnp.float32
    )
    centre = jnp.sum(grad_probs * probs, axis=3, keepdims=True)
    grad_scores = (probs * (grad_probs - centre) * scale_factor).astype(jnp.bfloat16)
    grad_source = jnp.einsum(
        "chrk,ckhd->crhd", grad_scores, neighbour_keys, preferred_element_type=jnp.float32
    )
    grad_source = grad_source.reshape(row_count, column_count).astype(jnp.bfloat16)
    grad_keys = jnp.einsum(
        "chrk,crhd->ckhd", grad_scores, queries, preferred_element_type=jnp.float32
    ).reshape(n_keys.shape)
    grad_values = jnp.einsum(
        "chrk,crhd->ckhd", probs_low, grad_rows, preferred_element_type=jnp.float32
    ).reshape(n_values.shape)
    carried = from_behind(grad_source[row_count - lag_rows :], ctx_count, 1)
    d_query = jnp.concatenate([carried, grad_source[: row_count - lag_rows]], axis=0)
    squares = jnp.sum(grad_keys * grad_keys) + jnp.sum(grad_values * grad_values)
    overall = lax.psum(squares, ("outer", "z", "head"))
    factor = lax.rsqrt(overall / element_total + 1e-06)
    d_keys = (grad_keys * factor).astype(jnp.bfloat16)
    d_values = (grad_values * factor).astype(jnp.bfloat16)
    return (cross_out, d_query, d_keys, d_values)


def solution(mesh):
    outer_count = mesh.shape["ctx"] // 8
    z_count = 8
    head_count = mesh.shape["head"]
    regrouped = Mesh(
        mesh.devices.reshape(outer_count, z_count, head_count), ("outer", "z", "head")
    )
    ctx_count = outer_count * z_count

    def body(q_self, k_self, v_self, q_cross, n_keys, n_values, d_cross):
        element_total = 2.0 * n_keys.size * ctx_count * head_count
        self_out = self_attention(q_self, k_self, v_self, outer_count, z_count)
        cross_out, d_query, d_keys, d_values = cross_attention(
            q_cross, n_keys, n_values, d_cross, ctx_count, element_total
        )
        return (self_out, cross_out, d_query, d_keys, d_values)

    spec = P(CTX, "head")
    return jax.shard_map(
        body, mesh=regrouped, in_specs=(spec,) * 7, out_specs=(spec,) * 5, check_vma=False
    )
```

time: 506 us -> 310 us (0.61)
  the two profiles are of different devices: /device:TPU:54 before, /device:TPU:1 now
where the time goes in v1:
time: 310 us; the launch traced here: 309 us
  blocking collectives  145 us (47%)
  waiting for transfers between devices  73.1 us (24%)
  starting transfers between devices  30.4 us (10%)
  matrix products  27.8 us (9%)
  local copies, waits for them, and re-layouts  16 us (5%)
  other arithmetic  14.4 us (5%)
    psum x1, blocking collectives, cross_attention(): overall = lax.psum(squares, ('outer', 'z', 'head'))  145 us
    all_to_all x2, waiting for transfers between devices, spread(): return lax.all_to_all(copies, axis, 0, 0, tiled=True)  73.1 us
    all_to_all x2, starting transfers between devices, spread(): return lax.all_to_all(copies, axis, 0, 0, tiled=True)  20.1 us
    dot_general x1, matrix products, self_attention(): jnp.einsum('hgrk,khd->grhd', weights.astype(jnp.bfloat16), values, prefer...  6.41 us
  transfers between devices with their start and end apart: 5, of which 2 were waited for; matrix products, arithmetic and copies ran while one was open for 12% of the time, Pallas kernels for 0%

profile of v1, /device:TPU:1, one launch (start us, length us, event | category | flops | bytes accessed | tf_op | source)
XLA Modules:
  0.0 309.3 jit_solution(4696943074475347295)
XLA Ops:
  1.8 1.6 broadcast_in_dim.22
  3.5 10.9 %all-to-all-start = ((bf16[8,128,1024]{1,2,0:T(8,128)(2,1)}), bf16[8,128,1024]{1,2,0:T(8,128)(2,1)S(1)}, u32[]{:S(2)}, u32[]{:S(2)}) async-start(bf16[8,128,1024]{1,2,0:T(8,128)(2,1)} %broadcast_in_dim.22), calls=%async_computation | async-start | bytes 4194304 | tf_op jit(solution)/shard_map/all_to_all | solution.py:21
  14.5 51.5 %all-to-all-done = bf16[8,128,1024]{1,2,0:T(8,128)(2,1)S(1)} async-done(((bf16[8,128,1024]{1,2,0:T(8,128)(2,1)}), bf16[8,128,1024]{1,2,0:T(8,128)(2,1)S(1)}, u32[]{:S(2)}, u32[]{:S(2)}) %all-to-all-start) | async-done | bytes 2097184 | tf_op jit(solution)/shard_map/all_to_all | solution.py:21
  67.1 9.3 %all-to-all-start.1 = ((bf16[8,128,512]{1,2,0:T(8,128)(2,1)}), bf16[8,128,512]{1,2,0:T(8,128)(2,1)}, u32[]{:S(2)}, u32[]{:S(2)}) async-start(bf16[8,128,512]{1,2,0:T(8,128)(2,1)} %broadcast_in_dim.24), calls=%async_computation.1 | async-start | bytes 2097152 | tf_op jit(solution)/shard_map/all_to_all | solution.py:21
  77.5 1.2 fusion.52
  78.7 21.6 %all-to-all-done.1 = bf16[8,128,512]{1,2,0:T(8,128)(2,1)} async-done(((bf16[8,128,512]{1,2,0:T(8,128)(2,1)}), bf16[8,128,512]{1,2,0:T(8,128)(2,1)}, u32[]{:S(2)}, u32[]{:S(2)}) %all-to-all-start.1) | async-done | bytes 1048608 | tf_op jit(solution)/shard_map/all_to_all | solution.py:21
  100.2 4.5 %fusion.2 = (f32[4,8,128]{2,1,0:T(8,128)S(1)}, f32[4,1024,8,128]{3,1,2,0:T(8,128)S(1)}) fusion(pred[8,128,1024]{1,2,0:T(8,128)(4,1)S(1)} %broadcast_compare_fusion, bf16[1024,4,128,1]{0,2,3,1:T(8,128)(2,1)S(1)} %bitcast.75, bf16[8,128,4,128]{1,3,2,0:T(8,128)(2,1)} %bitcast.5), kind=kOutput, calls=%fused_computation.4 | convolution fusion | flops 1086320640 | bytes 19939328 | tf_op jit(solution)/shard_map/grhd,khd->hgrk/dot_general | solution.py:39
  104.8 4.2 %fusion.3 = f32[4,8,128]{2,1,0:T(8,128)S(1)} fusion(f32[4,1024,8,128]{3,1,2,0:T(8,128)S(1)} %get-tuple-element.15, f32[4,8,128]{2,1,0:T(8,128)S(1)} %get-tuple-element.14, pred[8,128,1024]{1,2,0:T(8,128)(4,1)S(1)} %broadcast_compare_fusion), kind=kLoop, calls=%fused_computation.5 | loop fusion | flops 20967424 | bytes 17858560 | tf_op jit(solution)/shard_map/reduce_sum | solution.py:45
  109.0 6.4 %fusion.9 = f32[8,128,4,128]{1,3,0,2:T(8,128)S(1)} fusion(bf16[1024,4,128,1]{0,2,3,1:T(8,128)(2,1)} %bitcast.74, f32[4,1024,8,128]{3,1,2,0:T(8,128)S(1)} %get-tuple-element.15, f32[4,8,128]{2,1,0:T(8,128)S(1)} %get-tuple-element.14, pred[8,128,1024]{1,2,0:T(8,128)(4,1)S(1)} %broadcast_compare_fusion), kind=kOutput, calls=%fused_computation.14 | convolution fusion | flops 1094713344 | bytes 20987904 | tf_op jit(solution)/shard_map/hgrk,khd->grhd/dot_general | solution.py:46
  115.6 1.5 pad_maximum_fusion
  117.1 4.1 %all-to-all-start.2 = ((f32[8,128,520]{1,2,0:T(8,128)}), f32[8,128,520]{1,2,0:T(8,128)S(1)}, u32[]{:S(2)}, u32[]{:S(2)}) async-start(f32[8,128,520]{1,2,0:T(8,128)} %pad_maximum_fusion), calls=%async_computation.2 | async-start | bytes 4259840 | tf_op jit(solution)/shard_map/all_to_all | solution.py:53
  121.2 1.5 collective-permute-start
  124.9 2.0 reshape.102
  127.8 1.4 convolution_multiply_fusion
  130.1 4.9 %fusion.19 = bf16[2,64,4,128]{3,1,2,0:T(8,128)(2,1)} fusion(f32[2,4,64,256]{3,2,1,0:T(8,128)} %fusion.29, bf16[2,256,4,128]{3,2,1,0:T(4,128)(2,1)} %reshape.102, f32[2,4,64,256]{3,2,1,0:T(8,128)} %get-tuple-element.17, f32[2,4,64]{2,1,0:T(4,128)S(1)} %get-tuple-element.16), kind=kOutput, calls=%fused_computation.25 | convolution fusion | flops 34538240 | bytes 1705984 | tf_op jit(solution)/shard_map/chrk,ckhd->crhd/dot_general | solution.py:95
  136.1 2.9 multiply_reduce_fusion
  138.9 5.7 %multiply_reduce_fusion.1 = (f32[]{:T(128)}, f32[2,4,128,256]{3,2,1,0:T(8,128)}) fusion(f32[2,4,64,256]{3,2,1,0:T(8,128)} %fusion.29, f32[2,4,64,256]{3,2,1,0:T(8,128)} %get-tuple-element.17, f32[2,4,64]{2,1,0:T(4,128)S(1)} %get-tuple-element.16, bf16[2,64,4,128]{3,2,1,0:T(4,128)(2,1)} %copy-done), kind=kOutput, calls=%fused_computation.32 | convolution fusion | flops 34996992 | bytes 2230276 | tf_op jit(solution)/shard_map/chrk,crhd->ckhd/dot_general | solution.py:99
  146.0 4.6 %collective-permute-start.1 = (bf16[63,512]{1,0:T(8,128)(2,1)S(1)}, bf16[63,512]{1,0:T(8,128)(2,1)}, u32[]{:S(2)}, u32[]{:S(2)}) collective-permute-start(bf16[63,512]{1,0:T(8,128)(2,1)S(1)} %slice.41), channel_id=1, source_target_pairs={{0,8},{8,16},{16,24},{24,32},{32,40},{40,48},{48,56},{56,64},{64,7... | collective-permute-start | bytes 193544 | tf_op jit(solution)/shard_map/ppermute | solution.py:16
  150.6 144.7 %psum.7 = f32[]{:T(128)} all-reduce(f32[]{:T(128)S(6)} %add.52), channel_id=1, replica_groups=mesh['outer'=8,'z'=8,'head'=8] {'outer','z','head'}, use_global_device_ids=true, to_apply=%region_10.11 | all-reduce | flops 1 | bytes 8 | tf_op jit(solution)/shard_map/psum | solution.py:108
  296.0 1.3 fusion.28
  298.5 2.1 fusion.27
  300.6 2.1 copy.59
  302.7 2.3 copy_bitcast_fusion.1
  306.7 1.5 pad_maximum_fusion.3
  (44 shorter events, 12.7 us)
Async XLA Ops:
  0.6 13.7 %copy-start.3 = (bf16[128,512]{1,0:T(8,128)(2,1)S(1)}, bf16[128,512]{1,0:T(8,128)(2,1)}, u32[]{:S(2)}) copy-start(bf16[128,512]{1,0:T(8,128)(2,1)} %param.7) | copy-start | bytes 393220
  3.5 62.5 %all-to-all-start = ((bf16[8,128,1024]{1,2,0:T(8,128)(2,1)}), bf16[8,128,1024]{1,2,0:T(8,128)(2,1)S(1)}, u32[]{:S(2)}, u32[]{:S(2)}) async-start(bf16[8,128,1024]{1,2,0:T(8,128)(2,1)} %broadcast_in_dim.22), calls=%async_computation | async-start | bytes 4194304 | tf_op jit(solution)/shard_map/all_to_all | solution.py:21
  67.1 33.1 %all-to-all-start.1 = ((bf16[8,128,512]{1,2,0:T(8,128)(2,1)}), bf16[8,128,512]{1,2,0:T(8,128)(2,1)}, u32[]{:S(2)}, u32[]{:S(2)}) async-start(bf16[8,128,512]{1,2,0:T(8,128)(2,1)} %broadcast_in_dim.24), calls=%async_computation.1 | async-start | bytes 2097152 | tf_op jit(solution)/shard_map/all_to_all | solution.py:21
  115.5 5.7 %copy-start.2 = (bf16[128,512]{1,0:T(8,128)(2,1)S(1)}, bf16[128,512]{1,0:T(8,128)(2,1)}, u32[]{:S(2)}) copy-start(bf16[128,512]{1,0:T(8,128)(2,1)} %param.10) | copy-start | bytes 393220
  115.6 7.2 %copy-start.1 = (bf16[512,512]{1,0:T(8,128)(2,1)S(1)}, bf16[512,512]{1,0:T(8,128)(2,1)}, u32[]{:S(2)}) copy-start(bf16[512,512]{1,0:T(8,128)(2,1)} %param.12) | copy-start | bytes 1572868
  117.1 191.2 %all-to-all-start.2 = ((f32[8,128,520]{1,2,0:T(8,128)}), f32[8,128,520]{1,2,0:T(8,128)S(1)}, u32[]{:S(2)}, u32[]{:S(2)}) async-start(f32[8,128,520]{1,2,0:T(8,128)} %pad_maximum_fusion), calls=%async_computation.2 | async-start | bytes 4259840 | tf_op jit(solution)/shard_map/all_to_all | solution.py:53
  121.2 5.6 %collective-permute-start = (bf16[63,512]{1,0:T(8,128)(2,1)S(1)}, bf16[63,512]{1,0:T(8,128)(2,1)}, u32[]{:S(2)}, u32[]{:S(2)}) collective-permute-start(bf16[63,512]{1,0:T(8,128)(2,1)S(1)} %slice.33), channel_id=1, source_target_pairs={{8,0},{16,8},{24,16},{32,24},{40,32},{48,40},{56,48},{64,56},{72,6... | collective-permute-start | bytes 193544 | tf_op jit(solution)/shard_map/ppermute | solution.py:16
  127.8 8.2 %copy-start = (bf16[2,64,4,128]{3,2,1,0:T(4,128)(2,1)}, bf16[2,64,4,128]{3,2,1,0:T(4,128)(2,1)S(1)}, u32[]{:S(2)}) copy-start(bf16[2,64,4,128]{3,2,1,0:T(4,128)(2,1)S(1)} %reshape.101) | copy-start | bytes 393220
  146.0 160.8 %collective-permute-start.1 = (bf16[63,512]{1,0:T(8,128)(2,1)S(1)}, bf16[63,512]{1,0:T(8,128)(2,1)}, u32[]{:S(2)}, u32[]{:S(2)}) collective-permute-start(bf16[63,512]{1,0:T(8,128)(2,1)S(1)} %slice.41), channel_id=1, source_target_pairs={{0,8},{8,16},{16,24},{24,32},{32,40},{40,48},{48,56},{56,64},{64,7... | collective-permute-start | bytes 193544 | tf_op jit(solution)/shard_map/ppermute | solution.py:16

commit v2 on v1

--- a/solution.py
+++ b/solution.py
@@ -105,7 +105,11 @@
     carried = from_behind(grad_source[row_count - lag_rows :], ctx_count, 1)
     d_query = jnp.concatenate([carried, grad_source[: row_count - lag_rows]], axis=0)
     squares = jnp.sum(grad_keys * grad_keys) + jnp.sum(grad_values * grad_values)
-    overall = lax.psum(squares, ("outer", "z", "head"))
+    device_count = ctx_count * lax.axis_size("head")
+    every = lax.all_to_all(
+        jnp.broadcast_to(squares[None], (device_count,)), ("outer", "z", "head"), 0, 0, tiled=True
+    )
+    overall = jnp.sum(every)
     factor = lax.rsqrt(overall / element_total + 1e-06)
     d_keys = (grad_keys * factor).astype(jnp.bfloat16)
     d_values = (grad_values * factor).astype(jnp.bfloat16)

time: 310 us -> 201 us (0.65)
  the two profiles are of different devices: /device:TPU:1 before, /device:TPU:40 now
where the time goes in v2:
time: 201 us; the launch traced here: 200 us
  waiting for transfers between devices  80.3 us (40%)
  starting transfers between devices  54.1 us (27%)
  matrix products  31 us (15%)
  local copies, waits for them, and re-layouts  16.9 us (8%)
  other arithmetic  14.8 us (7%)
  between operations  2.92 us (1%)
    all_to_all x2, waiting for transfers between devices, spread(): return lax.all_to_all(copies, axis, 0, 0, tiled=True)  43.8 us
    ppermute x2, waiting for transfers between devices, from_behind(): return lax.ppermute(block, CTX, route)  36.5 us
    all_to_all x2, starting transfers between devices, spread(): return lax.all_to_all(copies, axis, 0, 0, tiled=True)  20 us
    all_to_all x1, starting transfers between devices, cross_attention(): lax.all_to_all(jnp.broadcast_to(squares[None], (device_count,)), ('outer'...  12.7 us
    ppermute x2, starting transfers between devices, from_behind(): return lax.ppermute(block, CTX, route)  11.7 us
    all_to_all x1, starting transfers between devices, self_attention(): back = lax.all_to_all(packed, 'outer', 0, 0, tiled=True)  9.77 us
    dot_general x1, matrix products, self_attention(): jnp.einsum('hgrk,khd->grhd', weights.astype(jnp.bfloat16), values, prefer...  6.42 us
    dot_general x1, matrix products, cross_attention(): jnp.einsum('chrk,crhd->ckhd', grad_scores, queries, preferred_element_typ...  5.68 us
  transfers between devices with their start and end apart: 6, of which 3 were waited for; matrix products, arithmetic and copies ran while one was open for 29% of the time, Pallas kernels for 0%

profile of v2, /device:TPU:40, one launch (start us, length us, event | category | flops | bytes accessed | tf_op | source)
XLA Modules:
  0.0 200.1 jit_solution(12652898420261780082)
XLA Ops:
  1.9 1.6 broadcast_in_dim.24
  3.5 10.3 %all-to-all-start = ((bf16[8,128,1024]{1,2,0:T(8,128)(2,1)}), bf16[8,128,1024]{1,2,0:T(8,128)(2,1)S(1)}, u32[]{:S(2)}, u32[]{:S(2)}) async-start(bf16[8,128,1024]{1,2,0:T(8,128)(2,1)} %broadcast_in_dim.24), calls=%async_computation | async-start | bytes 4194304 | tf_op jit(solution)/shard_map/all_to_all | solution.py:21
  14.5 7.8 %collective-permute-start = (bf16[63,512]{1,0:T(8,128)(2,1)}, bf16[63,512]{1,0:T(8,128)(2,1)}, u32[]{:S(2)}, u32[]{:S(2)}) collective-permute-start(bf16[63,512]{1,0:T(8,128)(2,1)} %slice.33), channel_id=1, source_target_pairs={{8,0},{16,8},{24,16},{32,24},{40,32},{48,40},{56,48},{64,56},{72,6... | collective-permute-start | bytes 193544 | tf_op jit(solution)/shard_map/ppermute | solution.py:16
  24.2 40.9 %all-to-all-done = bf16[8,128,1024]{1,2,0:T(8,128)(2,1)S(1)} async-done(((bf16[8,128,1024]{1,2,0:T(8,128)(2,1)}), bf16[8,128,1024]{1,2,0:T(8,128)(2,1)S(1)}, u32[]{:S(2)}, u32[]{:S(2)}) %all-to-all-start) | async-done | bytes 2097184 | tf_op jit(solution)/shard_map/all_to_all | solution.py:21
  66.2 9.7 %all-to-all-start.1 = ((bf16[8,128,512]{1,2,0:T(8,128)(2,1)}), bf16[8,128,512]{1,2,0:T(8,128)(2,1)}, u32[]{:S(2)}, u32[]{:S(2)}) async-start(bf16[8,128,512]{1,2,0:T(8,128)(2,1)} %broadcast_in_dim.26), calls=%async_computation.1 | async-start | bytes 2097152 | tf_op jit(solution)/shard_map/all_to_all | solution.py:21
  75.9 2.1 %fusion.29 = f32[2,4,64,256]{3,2,1,0:T(8,128)} fusion(bf16[2,256,4,128]{3,2,1,0:T(4,128)(2,1)} %reshape.106, bf16[2,64,4,128]{3,2,1,0:T(4,128)(2,1)S(1)} %reshape.107), kind=kOutput, calls=%fused_computation.40 | convolution fusion | flops 33554432 | bytes 1179648 | tf_op jit(solution)/shard_map/crhd,ckhd->chrk/dot_general | solution.py:90
  78.1 2.0 reshape.105
  80.9 1.3 convolution_multiply_fusion
  84.0 4.1 %multiply_reduce_fusion = (f32[]{:T(128)}, f32[2,4,256,128]{3,2,1,0:T(8,128)}) fusion(bf16[2,64,4,128]{3,2,1,0:T(4,128)(2,1)S(1)} %reshape.107, f32[2,4,64]{2,1,0:T(4,128)S(1)} %get-tuple-element.26, f32[2,4,64,256]{3,2,1,0:T(8,128)} %copy-done.1), kind=kOutput, calls=%fused_computation.31 | convolution fusion | flops 34472704 | bytes 1705988 | tf_op jit(solution)/shard_map/chrk,crhd->ckhd/dot_general | solution.py:102
  88.1 5.7 %multiply_reduce_fusion.1 = (f32[]{:T(128)}, f32[2,4,128,256]{3,2,1,0:T(8,128)}) fusion(f32[2,4,64,256]{3,2,1,0:T(8,128)} %fusion.29, f32[2,4,64,256]{3,2,1,0:T(8,128)} %get-tuple-element.27, f32[2,4,64]{2,1,0:T(4,128)S(1)} %get-tuple-element.26, bf16[2,64,4,128]{3,2,1,0:T(4,128)(2,1)S(1)} %reshape.104), kind=kOutput, calls=%fused_computation.32 | convolution fusion | flops 34996992 | bytes 2230276 | tf_op jit(solution)/shard_map/chrk,crhd->ckhd/dot_general | solution.py:99
  96.5 2.9 %all-to-all-done.1 = bf16[8,128,512]{1,2,0:T(8,128)(2,1)} async-done(((bf16[8,128,512]{1,2,0:T(8,128)(2,1)}), bf16[8,128,512]{1,2,0:T(8,128)(2,1)}, u32[]{:S(2)}, u32[]{:S(2)}) %all-to-all-start.1) | async-done | bytes 1048608 | tf_op jit(solution)/shard_map/all_to_all | solution.py:21
  100.3 12.7 %all-to-all-start.3 = ((f32[512,1,1]{2,1,0:T(1,128)}), f32[512,1,1]{2,1,0:T(1,128)S(1)}, u32[]{:S(2)}, u32[]{:S(2)}) async-start(f32[512,1,1]{2,1,0:T(1,128)} %broadcast_in_dim.29), calls=%async_computation.3 | async-start | bytes 524288 | tf_op jit(solution)/shard_map/all_to_all | solution.py:109
  113.0 4.5 %fusion.2 = (f32[4,8,128]{2,1,0:T(8,128)S(1)}, f32[4,1024,8,128]{3,1,2,0:T(8,128)S(1)}) fusion(pred[8,128,1024]{1,2,0:T(8,128)(4,1)S(1)} %broadcast_compare_fusion, bf16[1024,4,128,1]{0,2,3,1:T(8,128)(2,1)S(1)} %bitcast.75, bf16[8,128,4,128]{1,3,2,0:T(8,128)(2,1)} %bitcast.5), kind=kOutput, calls=%fused_computation.4 | convolution fusion | flops 1086320640 | bytes 19939328 | tf_op jit(solution)/shard_map/grhd,khd->hgrk/dot_general | solution.py:39
  117.5 4.2 %fusion.3 = f32[4,8,128]{2,1,0:T(8,128)S(1)} fusion(f32[4,1024,8,128]{3,1,2,0:T(8,128)S(1)} %get-tuple-element.25, f32[4,8,128]{2,1,0:T(8,128)S(1)} %get-tuple-element.24, pred[8,128,1024]{1,2,0:T(8,128)(4,1)S(1)} %broadcast_compare_fusion), kind=kLoop, calls=%fused_computation.5 | loop fusion | flops 20967424 | bytes 17858560 | tf_op jit(solution)/shard_map/reduce_sum | solution.py:45
  121.8 6.4 %fusion.9 = f32[8,128,4,128]{1,3,0,2:T(8,128)S(1)} fusion(bf16[1024,4,128,1]{0,2,3,1:T(8,128)(2,1)} %bitcast.74, f32[4,1024,8,128]{3,1,2,0:T(8,128)S(1)} %get-tuple-element.25, f32[4,8,128]{2,1,0:T(8,128)S(1)} %get-tuple-element.24, pred[8,128,1024]{1,2,0:T(8,128)(4,1)S(1)} %broadcast_compare_fusion), kind=kOutput, calls=%fused_computation.14 | convolution fusion | flops 1094713344 | bytes 20987904 | tf_op jit(solution)/shard_map/hgrk,khd->grhd/dot_general | solution.py:46
  128.4 1.5 pad_maximum_fusion
  129.9 9.8 %all-to-all-start.2 = ((f32[8,128,520]{1,2,0:T(8,128)}), f32[8,128,520]{1,2,0:T(8,128)S(1)}, u32[]{:S(2)}, u32[]{:S(2)}) async-start(f32[8,128,520]{1,2,0:T(8,128)} %pad_maximum_fusion), calls=%async_computation.2 | async-start | bytes 4259840 | tf_op jit(solution)/shard_map/all_to_all | solution.py:53
  139.7 4.7 %fusion.19 = bf16[2,64,4,128]{3,1,2,0:T(8,128)(2,1)} fusion(f32[2,4,64,256]{3,2,1,0:T(8,128)} %fusion.29, bf16[2,256,4,128]{3,2,1,0:T(4,128)(2,1)S(1)} %copy-done.2, f32[2,4,64,256]{3,2,1,0:T(8,128)} %get-tuple-element.27, f32[2,4,64]{2,1,0:T(4,128)S(1)} %get-tuple-element.26), kind=kOutput, calls=%fused_computation.25 | convolution fusion | flops 34538240 | bytes 1705984 | tf_op jit(solution)/shard_map/chrk,ckhd->crhd/dot_general | solution.py:95
  146.1 2.2 %fusion.18 = bf16[2,64,4,128]{3,1,2,0:T(8,128)(2,1)S(1)} fusion(bf16[2,256,4,128]{3,2,1,0:T(4,128)(2,1)S(1)} %copy-done, f32[2,4,64]{2,1,0:T(4,128)S(1)} %get-tuple-element.26, f32[2,4,64,256]{3,2,1,0:T(8,128)} %copy-done.1), kind=kOutput, calls=%fused_computation.24 | convolution fusion | flops 34013952 | bytes 1181696 | tf_op jit(solution)/shard_map/chrk,ckhd->crhd/dot_general | solution.py:86
  149.1 3.9 %collective-permute-start.1 = (bf16[63,512]{1,0:T(8,128)(2,1)}, bf16[63,512]{1,0:T(8,128)(2,1)}, u32[]{:S(2)}, u32[]{:S(2)}) collective-permute-start(bf16[63,512]{1,0:T(8,128)(2,1)} %slice.41), channel_id=1, source_target_pairs={{0,8},{8,16},{16,24},{24,32},{32,40},{40,48},{48,56},{56,64},{64,7... | collective-permute-start | bytes 193544 | tf_op jit(solution)/shard_map/ppermute | solution.py:16
  154.8 1.3 fusion.28
  158.9 2.2 %copy_bitcast_fusion.1 = (bf16[512,512]{1,0:T(8,128)(2,1)}, bf16[512,512]{1,0:T(8,128)(2,1)}) fusion(bf16[64,8,4,128]{3,2,1,0:T(4,128)(2,1)S(1)} %bitcast.72, bf16[64,8,4,128]{3,2,1,0:T(4,128)(2,1)} %bitcast.73), kind=kLoop, calls=%fused_computation.38 | loop fusion | bytes 2097152 | tf_op jit(solution)/shard_map/convert_element_type | solution.py:115
  161.1 36.5 %collective-permute-done.1 = bf16[63,512]{1,0:T(8,128)(2,1)} collective-permute-done((bf16[63,512]{1,0:T(8,128)(2,1)}, bf16[63,512]{1,0:T(8,128)(2,1)}, u32[]{:S(2)}, u32[]{:S(2)}) %collective-permute-start.1) | collective-permute-done | bytes 64544 | tf_op jit(solution)/shard_map/ppermute | solution.py:16
  197.6 1.5 pad_maximum_fusion.3
  (53 shorter events, 17.4 us)
Async XLA Ops:
  0.6 13.2 %copy-start.4 = (bf16[128,512]{1,0:T(8,128)(2,1)S(1)}, bf16[128,512]{1,0:T(8,128)(2,1)}, u32[]{:S(2)}) copy-start(bf16[128,512]{1,0:T(8,128)(2,1)} %param.10) | copy-start | bytes 393220
  0.6 21.6 %copy-start.5 = (bf16[128,512]{1,0:T(8,128)(2,1)S(1)}, bf16[128,512]{1,0:T(8,128)(2,1)}, u32[]{:S(2)}) copy-start(bf16[128,512]{1,0:T(8,128)(2,1)} %param.7) | copy-start | bytes 393220
  0.7 21.8 %copy-start.3 = (bf16[512,512]{1,0:T(8,128)(2,1)S(1)}, bf16[512,512]{1,0:T(8,128)(2,1)}, u32[]{:S(2)}) copy-start(bf16[512,512]{1,0:T(8,128)(2,1)} %param.12) | copy-start | bytes 1572868
  1.9 21.4 %copy-start.6 = (bf16[128,512]{1,0:T(8,128)(2,1)S(1)}, bf16[128,512]{1,0:T(8,128)(2,1)}, u32[]{:S(2)}) copy-start(bf16[128,512]{1,0:T(8,128)(2,1)} %param.13) | copy-start | bytes 393220
  3.5 61.5 %all-to-all-start = ((bf16[8,128,1024]{1,2,0:T(8,128)(2,1)}), bf16[8,128,1024]{1,2,0:T(8,128)(2,1)S(1)}, u32[]{:S(2)}, u32[]{:S(2)}) async-start(bf16[8,128,1024]{1,2,0:T(8,128)(2,1)} %broadcast_in_dim.24), calls=%async_computation | async-start | bytes 4194304 | tf_op jit(solution)/shard_map/all_to_all | solution.py:21
  14.5 65.5 %collective-permute-start = (bf16[63,512]{1,0:T(8,128)(2,1)}, bf16[63,512]{1,0:T(8,128)(2,1)}, u32[]{:S(2)}, u32[]{:S(2)}) collective-permute-start(bf16[63,512]{1,0:T(8,128)(2,1)} %slice.33), channel_id=1, source_target_pairs={{8,0},{16,8},{24,16},{32,24},{40,32},{48,40},{56,48},{64,56},{72,6... | collective-permute-start | bytes 193544 | tf_op jit(solution)/shard_map/ppermute | solution.py:16
  66.2 33.2 %all-to-all-start.1 = ((bf16[8,128,512]{1,2,0:T(8,128)(2,1)}), bf16[8,128,512]{1,2,0:T(8,128)(2,1)}, u32[]{:S(2)}, u32[]{:S(2)}) async-start(bf16[8,128,512]{1,2,0:T(8,128)(2,1)} %broadcast_in_dim.26), calls=%async_computation.1 | async-start | bytes 2097152 | tf_op jit(solution)/shard_map/all_to_all | solution.py:21
  82.3 0.8 copy-start.1
  100.3 29.7 %all-to-all-start.3 = ((f32[512,1,1]{2,1,0:T(1,128)}), f32[512,1,1]{2,1,0:T(1,128)S(1)}, u32[]{:S(2)}, u32[]{:S(2)}) async-start(f32[512,1,1]{2,1,0:T(1,128)} %broadcast_in_dim.29), calls=%async_computation.3 | async-start | bytes 524288 | tf_op jit(solution)/shard_map/all_to_all | solution.py:109
  128.4 11.3 %copy-start.2 = (bf16[2,256,4,128]{3,2,1,0:T(4,128)(2,1)S(1)}, bf16[2,256,4,128]{3,2,1,0:T(4,128)(2,1)}, u32[]{:S(2)}) copy-start(bf16[2,256,4,128]{3,2,1,0:T(4,128)(2,1)} %reshape.105) | copy-start | bytes 1572868
  129.9 16.2 %copy-start = (bf16[2,256,4,128]{3,2,1,0:T(4,128)(2,1)S(1)}, bf16[2,256,4,128]{3,2,1,0:T(4,128)(2,1)}, u32[]{:S(2)}) copy-start(bf16[2,256,4,128]{3,2,1,0:T(4,128)(2,1)} %reshape.106) | copy-start | bytes 1572868
  129.9 69.2 %all-to-all-start.2 = ((f32[8,128,520]{1,2,0:T(8,128)}), f32[8,128,520]{1,2,0:T(8,128)S(1)}, u32[]{:S(2)}, u32[]{:S(2)}) async-start(f32[8,128,520]{1,2,0:T(8,128)} %pad_maximum_fusion), calls=%async_computation.2 | async-start | bytes 4259840 | tf_op jit(solution)/shard_map/all_to_all | solution.py:53
  149.1 48.5 %collective-permute-start.1 = (bf16[63,512]{1,0:T(8,128)(2,1)}, bf16[63,512]{1,0:T(8,128)(2,1)}, u32[]{:S(2)}, u32[]{:S(2)}) collective-permute-start(bf16[63,512]{1,0:T(8,128)(2,1)} %slice.41), channel_id=1, source_target_pairs={{0,8},{8,16},{16,24},{24,32},{32,40},{40,48},{48,56},{56,64},{64,7... | collective-permute-start | bytes 193544 | tf_op jit(solution)/shard_map/ppermute | solution.py:16

commit v3 on v2

--- a/solution.py
+++ b/solution.py
@@ -45,19 +45,33 @@
     part_sum = jnp.sum(weights, axis=3)
     part_acc = jnp.einsum(
         "hgrk,khd->grhd", weights.astype(jnp.bfloat16), values, preferred_element_type=jnp.float32
-    ).reshape(outer_count, row_count, column_count)
-    stats = jnp.concatenate(
-        [part_max.transpose(1, 2, 0), part_sum.transpose(1, 2, 0)], axis=2
     )
-    packed = jnp.concatenate([part_acc, stats], axis=2)
+    present = part_sum > 0
+    inverse = jnp.where(present, 1.0 / jnp.where(present, part_sum, 1.0), 0.0)
+    part_out = (part_acc * inverse.transpose(1, 2, 0)[..., None]).astype(jnp.bfloat16)
+    level = jnp.where(present, part_max + jnp.log(jnp.where(present, part_sum, 1.0)), -1e30)
+    level = level.transpose(1, 2, 0)
+    pieces = []
+    rest = level
+    for unused in range(3):
+        piece = lax.optimization_barrier(rest.astype(jnp.bfloat16))
+        pieces.append(piece)
+        rest = rest - piece.astype(jnp.float32)
+    packed = jnp.concatenate(
+        [part_out.reshape(outer_count, row_count, column_count)] + pieces, axis=2
+    )
     back = lax.all_to_all(packed, "outer", 0, 0, tiled=True)
-    got_acc = back[:, :, :column_count].reshape(outer_count, row_count, head_count, HD)
-    got_max = back[:, :, column_count : column_count + head_count]
-    got_sum = back[:, :, column_count + head_count :]
-    top = jnp.max(got_max, axis=0)
-    rescale = jnp.exp(got_max - top[None])
-    total = jnp.sum(got_sum * rescale, axis=0)
-    mixed = jnp.sum(got_acc * rescale[..., None], axis=0)
+    got_out = back[:, :, :column_count].reshape(outer_count, row_count, head_count, HD)
+    got_level = sum(
+        back[:, :, column_count + i * head_count : column_count + (i + 1) * head_count].astype(
+            jnp.float32
+        )
+        for i in range(3)
+    )
+    top = jnp.max(got_level, axis=0)
+    rescale = jnp.exp(got_level - top[None])
+    total = jnp.sum(rescale, axis=0)
+    mixed = jnp.sum(got_out.astype(jnp.float32) * rescale[..., None], axis=0)
     out = mixed / total[..., None]
     return out.reshape(row_count, column_count).astype(jnp.bfloat16)
 

time: 201 us -> 176 us (0.88)
  waiting for transfers between devices: 80.3 us -> 61.6 us
  local copies, waits for them, and re-layouts: 16.9 us -> 14 us
    ppermute x2, waiting for transfers between devices: 36.5 us -> 16.9 us  [from_behind(): return lax.ppermute(block, CTX, route)]
where the time goes in v3:
time: 176 us; the launch traced here: 175 us
  waiting for transfers between devices  61.6 us (35%)
  starting transfers between devices  54 us (31%)
  matrix products  29.6 us (17%)
  local copies, waits for them, and re-layouts  14 us (8%)
  other arithmetic  13.3 us (8%)
  between operations  2.98 us (2%)
    all_to_all x2, waiting for transfers between devices, spread(): return lax.all_to_all(copies, axis, 0, 0, tiled=True)  44.7 us
    all_to_all x2, starting transfers between devices, spread(): return lax.all_to_all(copies, axis, 0, 0, tiled=True)  20 us
    ppermute x2, waiting for transfers between devices, from_behind(): return lax.ppermute(block, CTX, route)  16.9 us
    all_to_all x1, starting transfers between devices, cross_attention(): lax.all_to_all(jnp.broadcast_to(squares[None], (device_count,)), ('outer'...  12.7 us
    ppermute x2, starting transfers between devices, from_behind(): return lax.ppermute(block, CTX, route)  11.7 us
    all_to_all x1, starting transfers between devices, self_attention(): back = lax.all_to_all(packed, 'outer', 0, 0, tiled=True)  9.64 us
    dot_general x1, matrix products, cross_attention(): jnp.einsum('chrk,crhd->ckhd', grad_scores, queries, preferred_element_typ...  5.69 us
    dot_general x1, matrix products, self_attention(): jnp.einsum('hgrk,khd->grhd', weights.astype(jnp.bfloat16), values, prefer...  4.99 us
  transfers between devices with their start and end apart: 6, of which 3 were waited for; matrix products, arithmetic and copies ran while one was open for 29% of the time, Pallas kernels for 0%

profile of v3, /device:TPU:40, one launch (start us, length us, event | category | flops | bytes accessed | tf_op | source)
XLA Modules:
  0.0 175.5 jit_solution(14968071171329200696)
XLA Ops:
  1.9 1.6 broadcast_in_dim.31
  3.5 10.3 %all-to-all-start = ((bf16[8,128,1024]{1,2,0:T(8,128)(2,1)}), bf16[8,128,1024]{1,2,0:T(8,128)(2,1)S(1)}, u32[]{:S(2)}, u32[]{:S(2)}) async-start(bf16[8,128,1024]{1,2,0:T(8,128)(2,1)} %broadcast_in_dim.31), calls=%async_computation | async-start | bytes 4194304 | tf_op jit(solution)/shard_map/all_to_all | solution.py:21
  14.5 7.8 %collective-permute-start = (bf16[63,512]{1,0:T(8,128)(2,1)}, bf16[63,512]{1,0:T(8,128)(2,1)}, u32[]{:S(2)}, u32[]{:S(2)}) collective-permute-start(bf16[63,512]{1,0:T(8,128)(2,1)} %slice.37), channel_id=1, source_target_pairs={{8,0},{16,8},{24,16},{32,24},{40,32},{48,40},{56,48},{64,56},{72,6... | collective-permute-start | bytes 193544 | tf_op jit(solution)/shard_map/ppermute | solution.py:16
  24.2 40.9 %all-to-all-done = bf16[8,128,1024]{1,2,0:T(8,128)(2,1)S(1)} async-done(((bf16[8,128,1024]{1,2,0:T(8,128)(2,1)}), bf16[8,128,1024]{1,2,0:T(8,128)(2,1)S(1)}, u32[]{:S(2)}, u32[]{:S(2)}) %all-to-all-start) | async-done | bytes 2097184 | tf_op jit(solution)/shard_map/all_to_all | solution.py:21
  66.2 9.7 %all-to-all-start.1 = ((bf16[8,128,512]{1,2,0:T(8,128)(2,1)}), bf16[8,128,512]{1,2,0:T(8,128)(2,1)}, u32[]{:S(2)}, u32[]{:S(2)}) async-start(bf16[8,128,512]{1,2,0:T(8,128)(2,1)} %broadcast_in_dim.33), calls=%async_computation.1 | async-start | bytes 2097152 | tf_op jit(solution)/shard_map/all_to_all | solution.py:21
  75.8 2.1 %fusion.29 = f32[2,4,64,256]{3,2,1,0:T(8,128)} fusion(bf16[2,256,4,128]{3,2,1,0:T(4,128)(2,1)} %reshape.107, bf16[2,64,4,128]{3,2,1,0:T(4,128)(2,1)S(1)} %reshape.108), kind=kOutput, calls=%fused_computation.41 | convolution fusion | flops 33554432 | bytes 1179648 | tf_op jit(solution)/shard_map/crhd,ckhd->chrk/dot_general | solution.py:104
  78.0 2.0 %reshape.106 = bf16[2,256,4,128]{3,2,1,0:T(4,128)(2,1)} reshape(bf16[512,512]{1,0:T(8,128)(2,1)} %param.11) | data formatting | bytes 1048576 | tf_op jit(solution)/shard_map/reshape | solution.py:89
  80.9 1.3 convolution_multiply_fusion
  84.0 4.1 %multiply_reduce_fusion = (f32[]{:T(128)}, f32[2,4,256,128]{3,2,1,0:T(8,128)}) fusion(bf16[2,64,4,128]{3,2,1,0:T(4,128)(2,1)S(1)} %reshape.108, f32[2,4,64]{2,1,0:T(4,128)S(1)} %get-tuple-element.28, f32[2,4,64,256]{3,2,1,0:T(8,128)} %copy-done.1), kind=kOutput, calls=%fused_computation.32 | convolution fusion | flops 34472704 | bytes 1705988 | tf_op jit(solution)/shard_map/chrk,crhd->ckhd/dot_general | solution.py:116
  88.1 5.7 %multiply_reduce_fusion.1 = (f32[]{:T(128)}, f32[2,4,128,256]{3,2,1,0:T(8,128)}) fusion(f32[2,4,64,256]{3,2,1,0:T(8,128)} %fusion.29, f32[2,4,64,256]{3,2,1,0:T(8,128)} %get-tuple-element.29, f32[2,4,64]{2,1,0:T(4,128)S(1)} %get-tuple-element.28, bf16[2,64,4,128]{3,2,1,0:T(4,128)(2,1)S(1)} %reshape.105), kind=kOutput, calls=%fused_computation.33 | convolution fusion | flops 34996992 | bytes 2230276 | tf_op jit(solution)/shard_map/chrk,crhd->ckhd/dot_general | solution.py:113
  95.6 3.8 %all-to-all-done.1 = bf16[8,128,512]{1,2,0:T(8,128)(2,1)} async-done(((bf16[8,128,512]{1,2,0:T(8,128)(2,1)}), bf16[8,128,512]{1,2,0:T(8,128)(2,1)}, u32[]{:S(2)}, u32[]{:S(2)}) %all-to-all-start.1) | async-done | bytes 1048608 | tf_op jit(solution)/shard_map/all_to_all | solution.py:21
  100.2 12.7 %all-to-all-start.3 = ((f32[512,1,1]{2,1,0:T(1,128)}), f32[512,1,1]{2,1,0:T(1,128)S(1)}, u32[]{:S(2)}, u32[]{:S(2)}) async-start(f32[512,1,1]{2,1,0:T(1,128)} %broadcast_in_dim.62), calls=%async_computation.3 | async-start | bytes 524288 | tf_op jit(solution)/shard_map/all_to_all | solution.py:123
  112.9 4.5 %fusion.2 = (f32[4,8,128]{2,1,0:T(8,128)S(1)}, f32[4,1024,8,128]{3,1,2,0:T(8,128)S(1)}) fusion(pred[8,128,1024]{1,2,0:T(8,128)(4,1)S(1)} %broadcast_compare_fusion, bf16[1024,4,128,1]{0,2,3,1:T(8,128)(2,1)S(1)} %bitcast.104, bf16[8,128,4,128]{1,3,2,0:T(8,128)(2,1)} %bitcast.5), kind=kOutput, calls=%fused_computation.4 | convolution fusion | flops 1086320640 | bytes 19939328 | tf_op jit(solution)/shard_map/grhd,khd->hgrk/dot_general | solution.py:39
  117.4 4.2 %fusion.3 = f32[4,8,128]{2,1,0:T(8,128)S(1)} fusion(f32[4,1024,8,128]{3,1,2,0:T(8,128)S(1)} %get-tuple-element.27, f32[4,8,128]{2,1,0:T(8,128)S(1)} %get-tuple-element.26, pred[8,128,1024]{1,2,0:T(8,128)(4,1)S(1)} %broadcast_compare_fusion), kind=kLoop, calls=%fused_computation.5 | loop fusion | flops 20967424 | bytes 17858560 | tf_op jit(solution)/shard_map/reduce_sum | solution.py:45
  121.7 5.0 %fusion.9 = bf16[8,128,4,128]{1,3,0,2:T(8,128)(2,1)S(1)} fusion(bf16[1024,4,128,1]{0,2,3,1:T(8,128)(2,1)S(1)} %bitcast.103, f32[4,1024,8,128]{3,1,2,0:T(8,128)S(1)} %get-tuple-element.27, f32[4,8,128]{2,1,0:T(8,128)S(1)} %get-tuple-element.26, pred[8,128,1024]{1,2,0:T(8,128)(4,1)S(1)} %broadcast_compare_fusion, f32[8,128,4]{1,0,2:T(8,128)S(1)} %get-tuple-element.24), kind=kOutput, calls=%fused_computation.13 | convolution fusion | flops 1095761920 | bytes 19955712 | tf_op jit(solution)/shard_map/hgrk,khd->grhd/dot_general | solution.py:46
  127.9 9.6 %all-to-all-start.2 = ((bf16[8,128,524]{1,2,0:T(8,128)(2,1)}), bf16[8,128,524]{1,2,0:T(8,128)(2,1)S(1)}, u32[]{:S(2)}, u32[]{:S(2)}) async-start(bf16[8,128,524]{1,2,0:T(8,128)(2,1)} %pad_maximum_fusion), calls=%async_computation.2 | async-start | bytes 2162688 | tf_op jit(solution)/shard_map/all_to_all | solution.py:63
  137.6 4.7 %fusion.19 = bf16[2,64,4,128]{3,1,2,0:T(8,128)(2,1)} fusion(f32[2,4,64,256]{3,2,1,0:T(8,128)} %fusion.29, bf16[2,256,4,128]{3,2,1,0:T(4,128)(2,1)S(1)} %copy-done.2, f32[2,4,64,256]{3,2,1,0:T(8,128)} %get-tuple-element.29, f32[2,4,64]{2,1,0:T(4,128)S(1)} %get-tuple-element.28), kind=kOutput, calls=%fused_computation.25 | convolution fusion | flops 34538240 | bytes 1705984 | tf_op jit(solution)/shard_map/chrk,ckhd->crhd/dot_general | solution.py:109
  144.1 3.9 %collective-permute-start.1 = (bf16[63,512]{1,0:T(8,128)(2,1)}, bf16[63,512]{1,0:T(8,128)(2,1)}, u32[]{:S(2)}, u32[]{:S(2)}) collective-permute-start(bf16[63,512]{1,0:T(8,128)(2,1)} %slice.46), channel_id=1, source_target_pairs={{0,8},{8,16},{16,24},{24,32},{32,40},{40,48},{48,56},{56,64},{64,7... | collective-permute-start | bytes 193544 | tf_op jit(solution)/shard_map/ppermute | solution.py:16
  148.0 2.2 %fusion.18 = bf16[2,64,4,128]{3,1,2,0:T(8,128)(2,1)S(1)} fusion(bf16[2,256,4,128]{3,2,1,0:T(4,128)(2,1)S(1)} %copy-done, f32[2,4,64]{2,1,0:T(4,128)S(1)} %get-tuple-element.28, f32[2,4,64,256]{3,2,1,0:T(8,128)} %copy-done.1), kind=kOutput, calls=%fused_computation.24 | convolution fusion | flops 34013952 | bytes 1181696 | tf_op jit(solution)/shard_map/chrk,ckhd->crhd/dot_general | solution.py:100
  150.9 1.1 reduce_sum.82
  152.8 1.3 fusion.27
  154.9 1.1 copy_bitcast_fusion.1
  156.0 16.9 %collective-permute-done.1 = bf16[63,512]{1,0:T(8,128)(2,1)} collective-permute-done((bf16[63,512]{1,0:T(8,128)(2,1)}, bf16[63,512]{1,0:T(8,128)(2,1)}, u32[]{:S(2)}, u32[]{:S(2)}) %collective-permute-start.1) | collective-permute-done | bytes 64544 | tf_op jit(solution)/shard_map/ppermute | solution.py:16
  172.9 1.5 pad_maximum_fusion.3
  (59 shorter events, 14.5 us)
Async XLA Ops:
  0.6 13.2 %copy-start.5 = (bf16[128,512]{1,0:T(8,128)(2,1)S(1)}, bf16[128,512]{1,0:T(8,128)(2,1)}, u32[]{:S(2)}) copy-start(bf16[128,512]{1,0:T(8,128)(2,1)} %param.10) | copy-start | bytes 393220
  0.6 21.6 %copy-start.6 = (bf16[128,512]{1,0:T(8,128)(2,1)S(1)}, bf16[128,512]{1,0:T(8,128)(2,1)}, u32[]{:S(2)}) copy-start(bf16[128,512]{1,0:T(8,128)(2,1)} %param.7) | copy-start | bytes 393220
  0.7 21.8 %copy-start.4 = (bf16[512,512]{1,0:T(8,128)(2,1)S(1)}, bf16[512,512]{1,0:T(8,128)(2,1)}, u32[]{:S(2)}) copy-start(bf16[512,512]{1,0:T(8,128)(2,1)} %param.12) | copy-start | bytes 1572868
  1.9 21.4 %copy-start.7 = (bf16[128,512]{1,0:T(8,128)(2,1)S(1)}, bf16[128,512]{1,0:T(8,128)(2,1)}, u32[]{:S(2)}) copy-start(bf16[128,512]{1,0:T(8,128)(2,1)} %param.13) | copy-start | bytes 393220
  3.5 61.5 %all-to-all-start = ((bf16[8,128,1024]{1,2,0:T(8,128)(2,1)}), bf16[8,128,1024]{1,2,0:T(8,128)(2,1)S(1)}, u32[]{:S(2)}, u32[]{:S(2)}) async-start(bf16[8,128,1024]{1,2,0:T(8,128)(2,1)} %broadcast_in_dim.31), calls=%async_computation | async-start | bytes 4194304 | tf_op jit(solution)/shard_map/all_to_all | solution.py:21
  14.5 65.5 %collective-permute-start = (bf16[63,512]{1,0:T(8,128)(2,1)}, bf16[63,512]{1,0:T(8,128)(2,1)}, u32[]{:S(2)}, u32[]{:S(2)}) collective-permute-start(bf16[63,512]{1,0:T(8,128)(2,1)} %slice.37), channel_id=1, source_target_pairs={{8,0},{16,8},{24,16},{32,24},{40,32},{48,40},{56,48},{64,56},{72,6... | collective-permute-start | bytes 193544 | tf_op jit(solution)/shard_map/ppermute | solution.py:16
  66.2 33.2 %all-to-all-start.1 = ((bf16[8,128,512]{1,2,0:T(8,128)(2,1)}), bf16[8,128,512]{1,2,0:T(8,128)(2,1)}, u32[]{:S(2)}, u32[]{:S(2)}) async-start(bf16[8,128,512]{1,2,0:T(8,128)(2,1)} %broadcast_in_dim.33), calls=%async_computation.1 | async-start | bytes 2097152 | tf_op jit(solution)/shard_map/all_to_all | solution.py:21
  82.2 0.8 copy-start.1
  100.2 27.7 %all-to-all-start.3 = ((f32[512,1,1]{2,1,0:T(1,128)}), f32[512,1,1]{2,1,0:T(1,128)S(1)}, u32[]{:S(2)}, u32[]{:S(2)}) async-start(f32[512,1,1]{2,1,0:T(1,128)} %broadcast_in_dim.62), calls=%async_computation.3 | async-start | bytes 524288 | tf_op jit(solution)/shard_map/all_to_all | solution.py:123
  126.7 10.8 %copy-start.2 = (bf16[2,256,4,128]{3,2,1,0:T(4,128)(2,1)S(1)}, bf16[2,256,4,128]{3,2,1,0:T(4,128)(2,1)}, u32[]{:S(2)}) copy-start(bf16[2,256,4,128]{3,2,1,0:T(4,128)(2,1)} %reshape.106) | copy-start | bytes 1572868
  126.8 21.1 %copy-start = (bf16[2,256,4,128]{3,2,1,0:T(4,128)(2,1)S(1)}, bf16[2,256,4,128]{3,2,1,0:T(4,128)(2,1)}, u32[]{:S(2)}) copy-start(bf16[2,256,4,128]{3,2,1,0:T(4,128)(2,1)} %reshape.107) | copy-start | bytes 1572868
  127.9 46.5 %all-to-all-start.2 = ((bf16[8,128,524]{1,2,0:T(8,128)(2,1)}), bf16[8,128,524]{1,2,0:T(8,128)(2,1)S(1)}, u32[]{:S(2)}, u32[]{:S(2)}) async-start(bf16[8,128,524]{1,2,0:T(8,128)(2,1)} %pad_maximum_fusion), calls=%async_computation.2 | async-start | bytes 2162688 | tf_op jit(solution)/shard_map/all_to_all | solution.py:63
  142.3 12.1 %copy-start.3 = (f32[2,4,256,128]{3,2,1,0:T(8,128)S(1)}, f32[2,4,256,128]{3,2,1,0:T(8,128)}, u32[]{:S(2)}) copy-start(f32[2,4,256,128]{3,2,1,0:T(8,128)} %get-tuple-element.33) | copy-start | bytes 3145732
  144.1 28.8 %collective-permute-start.1 = (bf16[63,512]{1,0:T(8,128)(2,1)}, bf16[63,512]{1,0:T(8,128)(2,1)}, u32[]{:S(2)}, u32[]{:S(2)}) collective-permute-start(bf16[63,512]{1,0:T(8,128)(2,1)} %slice.46), channel_id=1, source_target_pairs={{0,8},{8,16},{16,24},{24,32},{32,40},{40,48},{48,56},{56,64},{64,7... | collective-permute-start | bytes 193544 | tf_op jit(solution)/shard_map/ppermute | solution.py:16

commit v4 on v3

--- a/solution.py
+++ b/solution.py
@@ -119,11 +119,13 @@
     carried = from_behind(grad_source[row_count - lag_rows :], ctx_count, 1)
     d_query = jnp.concatenate([carried, grad_source[: row_count - lag_rows]], axis=0)
     squares = jnp.sum(grad_keys * grad_keys) + jnp.sum(grad_values * grad_values)
-    device_count = ctx_count * lax.axis_size("head")
-    every = lax.all_to_all(
-        jnp.broadcast_to(squares[None], (device_count,)), ("outer", "z", "head"), 0, 0, tiled=True
-    )
-    overall = jnp.sum(every)
+    overall = squares
+    for axis in ("head", "z", "outer"):
+        count = lax.axis_size(axis)
+        bit = 1
+        while bit < count:
+            overall = overall + lax.ppermute(overall, axis, [(i, i ^ bit) for i in range(count)])
+            bit *= 2
     factor = lax.rsqrt(overall / element_total + 1e-06)
     d_keys = (grad_keys * factor).astype(jnp.bfloat16)
     d_values = (grad_values * factor).astype(jnp.bfloat16)

time: 176 us -> 213 us (1.21)
  starting transfers between devices: 54 us -> 76.1 us
  waiting for transfers between devices: 61.6 us -> 75.1 us
  between operations: 2.98 us -> 7.94 us
  matrix products: 29.6 us -> 27 us
    ppermute x0 -> x9, starting transfers between devices: none -> 36.4 us  [cross_attention(): lax.ppermute(overall, axis, [(i, i ^ bit) for i in range(count)])]
    ppermute x0 -> x9, waiting for transfers between devices: none -> 21.1 us  [cross_attention(): lax.ppermute(overall, axis, [(i, i ^ bit) for i in range(count)])]
    ppermute x2, waiting for transfers between devices: 16.9 us -> 0.01 us  [from_behind(): return lax.ppermute(block, CTX, route)]
    all_to_all x1 -> x0, starting transfers between devices: 12.7 us -> none  [cross_attention(): lax.all_to_all(jnp.broadcast_to(squares[None], (device_count,)), ('outer'...]
    all_to_all x2, waiting for transfers between devices: 44.7 us -> 54 us  [spread(): return lax.all_to_all(copies, axis, 0, 0, tiled=True)]
  transfers between devices with their start and end apart: 6 -> 14, of which waited for: 3 -> 11; matrix products, arithmetic and copies ran while one was open for 29% -> 15% of each run, Pallas kernels for 0% -> 0%
where the time goes in v4:
time: 213 us; the launch traced here: 211 us
  starting transfers between devices  76.1 us (36%)
  waiting for transfers between devices  75.1 us (35%)
  matrix products  27 us (13%)
  local copies, waits for them, and re-layouts  13.4 us (6%)
  other arithmetic  11.6 us (5%)
  between operations  7.94 us (4%)
    all_to_all x2, waiting for transfers between devices, spread(): return lax.all_to_all(copies, axis, 0, 0, tiled=True)  54 us
    ppermute x9, starting transfers between devices, cross_attention(): lax.ppermute(overall, axis, [(i, i ^ bit) for i in range(count)])  36.4 us
    ppermute x9, waiting for transfers between devices, cross_attention(): lax.ppermute(overall, axis, [(i, i ^ bit) for i in range(count)])  21.1 us
    all_to_all x2, starting transfers between devices, spread(): return lax.all_to_all(copies, axis, 0, 0, tiled=True)  20.1 us
    ppermute x2, starting transfers between devices, from_behind(): return lax.ppermute(block, CTX, route)  9.87 us
    all_to_all x1, starting transfers between devices, self_attention(): back = lax.all_to_all(packed, 'outer', 0, 0, tiled=True)  9.74 us
    dot_general x1, matrix products, self_attention(): jnp.einsum('hgrk,khd->grhd', weights.astype(jnp.bfloat16), values, prefer...  5 us
    dot_general x1, matrix products, cross_attention(): jnp.einsum('chrk,crhd->ckhd', grad_scores, queries, preferred_element_typ...  4.72 us
  transfers between devices with their start and end apart: 14, of which 11 were waited for; matrix products, arithmetic and copies ran while one was open for 15% of the time, Pallas kernels for 0%

profile of v4, /device:TPU:40, one launch (start us, length us, event | category | flops | bytes accessed | tf_op | source)
XLA Modules:
  0.0 211.1 jit_solution(15442970390174401089)
XLA Ops:
  3.5 10.4 %all-to-all-start = ((bf16[8,128,1024]{1,2,0:T(8,128)(2,1)}), bf16[8,128,1024]{1,2,0:T(8,128)(2,1)S(1)}, u32[]{:S(2)}, u32[]{:S(2)}) async-start(bf16[8,128,1024]{1,2,0:T(8,128)(2,1)} %broadcast_in_dim.29), calls=%async_computation | async-start | bytes 4194304 | tf_op jit(solution)/shard_map/all_to_all | solution.py:21
  14.0 7.8 %collective-permute-start = (bf16[63,512]{1,0:T(8,128)(2,1)S(1)}, bf16[63,512]{1,0:T(8,128)(2,1)}, u32[]{:S(2)}, u32[]{:S(2)}) collective-permute-start(bf16[63,512]{1,0:T(8,128)(2,1)S(1)} %slice.37), channel_id=1, source_target_pairs={{8,0},{16,8},{24,16},{32,24},{40,32},{48,40},{56,48},{64,56},{72,6... | collective-permute-start | bytes 193544 | tf_op jit(solution)/shard_map/ppermute | solution.py:16
  22.0 43.2 %all-to-all-done = bf16[8,128,1024]{1,2,0:T(8,128)(2,1)S(1)} async-done(((bf16[8,128,1024]{1,2,0:T(8,128)(2,1)}), bf16[8,128,1024]{1,2,0:T(8,128)(2,1)S(1)}, u32[]{:S(2)}, u32[]{:S(2)}) %all-to-all-start) | async-done | bytes 2097184 | tf_op jit(solution)/shard_map/all_to_all | solution.py:21
  66.3 9.7 %all-to-all-start.1 = ((bf16[8,128,512]{1,2,0:T(8,128)(2,1)}), bf16[8,128,512]{1,2,0:T(8,128)(2,1)}, u32[]{:S(2)}, u32[]{:S(2)}) async-start(bf16[8,128,512]{1,2,0:T(8,128)(2,1)} %broadcast_in_dim.52), calls=%async_computation.1 | async-start | bytes 2097152 | tf_op jit(solution)/shard_map/all_to_all | solution.py:21
  88.7 10.8 %all-to-all-done.1 = bf16[8,128,512]{1,2,0:T(8,128)(2,1)} async-done(((bf16[8,128,512]{1,2,0:T(8,128)(2,1)}), bf16[8,128,512]{1,2,0:T(8,128)(2,1)}, u32[]{:S(2)}, u32[]{:S(2)}) %all-to-all-start.1) | async-done | bytes 1048608 | tf_op jit(solution)/shard_map/all_to_all | solution.py:21
  99.5 4.5 %fusion.2 = (f32[4,8,128]{2,1,0:T(8,128)S(1)}, f32[4,1024,8,128]{3,1,2,0:T(8,128)S(1)}) fusion(pred[8,128,1024]{1,2,0:T(8,128)(4,1)S(1)} %broadcast_compare_fusion, bf16[1024,4,128,1]{0,2,3,1:T(8,128)(2,1)S(1)} %bitcast.104, bf16[8,128,4,128]{1,3,2,0:T(8,128)(2,1)} %bitcast.5), kind=kOutput, calls=%fused_computation.4 | convolution fusion | flops 1086320640 | bytes 19939328 | tf_op jit(solution)/shard_map/grhd,khd->hgrk/dot_general | solution.py:39
  104.0 4.2 %fusion.3 = f32[4,8,128]{2,1,0:T(8,128)S(1)} fusion(f32[4,1024,8,128]{3,1,2,0:T(8,128)S(1)} %get-tuple-element.17, f32[4,8,128]{2,1,0:T(8,128)S(1)} %get-tuple-element.16, pred[8,128,1024]{1,2,0:T(8,128)(4,1)S(1)} %broadcast_compare_fusion), kind=kLoop, calls=%fused_computation.5 | loop fusion | flops 20967424 | bytes 17858560 | tf_op jit(solution)/shard_map/reduce_sum | solution.py:45
  108.3 5.0 %fusion.9 = bf16[8,128,4,128]{1,3,0,2:T(8,128)(2,1)S(1)} fusion(bf16[1024,4,128,1]{0,2,3,1:T(8,128)(2,1)S(1)} %bitcast.103, f32[4,1024,8,128]{3,1,2,0:T(8,128)S(1)} %get-tuple-element.17, f32[4,8,128]{2,1,0:T(8,128)S(1)} %get-tuple-element.16, pred[8,128,1024]{1,2,0:T(8,128)(4,1)S(1)} %broadcast_compare_fusion, f32[8,128,4]{1,0,2:T(8,128)S(1)} %get-tuple-element.14), kind=kOutput, calls=%fused_computation.13 | convolution fusion | flops 1095761920 | bytes 19955712 | tf_op jit(solution)/shard_map/hgrk,khd->grhd/dot_general | solution.py:46
  114.5 9.7 %all-to-all-start.2 = ((bf16[8,128,524]{1,2,0:T(8,128)(2,1)}), bf16[8,128,524]{1,2,0:T(8,128)(2,1)S(1)}, u32[]{:S(2)}, u32[]{:S(2)}) async-start(bf16[8,128,524]{1,2,0:T(8,128)(2,1)} %pad_maximum_fusion), calls=%async_computation.2 | async-start | bytes 2162688 | tf_op jit(solution)/shard_map/all_to_all | solution.py:63
  124.3 4.1 %fusion.19 = bf16[2,64,4,128]{3,1,2,0:T(8,128)(2,1)S(1)} fusion(f32[2,4,64,256]{3,2,1,0:T(8,128)} %fusion.29, bf16[2,256,4,128]{3,2,1,0:T(4,128)(2,1)S(1)} %copy-done.2, f32[2,4,64,256]{3,2,1,0:T(8,128)} %get-tuple-element.19, f32[2,4,64]{2,1,0:T(4,128)S(1)} %get-tuple-element.18), kind=kOutput, calls=%fused_computation.25 | convolution fusion | flops 34538240 | bytes 1705984 | tf_op jit(solution)/shard_map/chrk,ckhd->crhd/dot_general | solution.py:109
  134.2 3.1 %multiply_reduce_fusion = (f32[]{:T(128)}, f32[2,4,256,128]{3,2,1,0:T(8,128)S(1)}) fusion(bf16[2,64,4,128]{3,2,1,0:T(4,128)(2,1)S(1)} %reshape.105, f32[2,4,64]{2,1,0:T(4,128)S(1)} %get-tuple-element.18, f32[2,4,64,256]{3,2,1,0:T(8,128)} %copy-done.1), kind=kOutput, calls=%fused_computation.32 | convolution fusion | flops 34472704 | bytes 1705988 | tf_op jit(solution)/shard_map/chrk,crhd->ckhd/dot_general | solution.py:116
  137.3 4.7 %multiply_reduce_fusion.1 = (f32[]{:T(128)}, f32[2,4,128,256]{3,2,1,0:T(8,128)S(1)}) fusion(f32[2,4,64,256]{3,2,1,0:T(8,128)} %fusion.29, f32[2,4,64,256]{3,2,1,0:T(8,128)} %get-tuple-element.19, f32[2,4,64]{2,1,0:T(4,128)S(1)} %get-tuple-element.18, bf16[2,64,4,128]{3,2,1,0:T(4,128)(2,1)S(1)} %reshape.102), kind=kOutput, calls=%fused_computation.33 | convolution fusion | flops 34996992 | bytes 2230276 | tf_op jit(solution)/shard_map/chrk,crhd->ckhd/dot_general | solution.py:113
  146.9 3.2 %collective-permute-start.3 = (f32[]{:T(128)}, f32[]{:T(128)}, u32[]{:S(2)}, u32[]{:S(2)}) collective-permute-start(f32[]{:T(128)} %add.91), channel_id=1, source_target_pairs={{0,2},{1,3},{2,0},{3,1},{4,6},{5,7},{6,4},{7,5},{8,10},{9,11},{10,... | collective-permute-start | bytes 20 | tf_op jit(solution)/shard_map/ppermute | solution.py:127
  153.0 3.5 %collective-permute-start.4 = (f32[]{:T(128)}, f32[]{:T(128)}, u32[]{:S(2)}, u32[]{:S(2)}) collective-permute-start(f32[]{:T(128)} %add.92), channel_id=1, source_target_pairs={{0,4},{1,5},{2,6},{3,7},{4,0},{5,1},{6,2},{7,3},{8,12},{9,13},{10,... | collective-permute-start | bytes 20 | tf_op jit(solution)/shard_map/ppermute | solution.py:127
  156.4 2.9 %collective-permute-done.4 = f32[]{:T(128)} collective-permute-done((f32[]{:T(128)}, f32[]{:T(128)}, u32[]{:S(2)}, u32[]{:S(2)}) %collective-permute-start.4) | collective-permute-done | bytes 36 | tf_op jit(solution)/shard_map/ppermute | solution.py:127
  159.9 3.4 %collective-permute-start.5 = (f32[]{:T(128)}, f32[]{:T(128)}, u32[]{:S(2)}, u32[]{:S(2)}) collective-permute-start(f32[]{:T(128)} %add.93), channel_id=1, source_target_pairs={{0,8},{8,0},{16,24},{24,16},{32,40},{40,32},{48,56},{56,48},{1,9},... | collective-permute-start | bytes 20 | tf_op jit(solution)/shard_map/ppermute | solution.py:127
  166.0 3.2 %collective-permute-start.6 = (f32[]{:T(128)}, f32[]{:T(128)}, u32[]{:S(2)}, u32[]{:S(2)}) collective-permute-start(f32[]{:T(128)} %add.94), channel_id=1, source_target_pairs={{0,16},{8,24},{16,0},{24,8},{32,48},{40,56},{48,32},{56,40},{1,17}... | collective-permute-start | bytes 20 | tf_op jit(solution)/shard_map/ppermute | solution.py:127
  169.2 3.1 %collective-permute-done.6 = f32[]{:T(128)} collective-permute-done((f32[]{:T(128)}, f32[]{:T(128)}, u32[]{:S(2)}, u32[]{:S(2)}) %collective-permute-start.6) | collective-permute-done | bytes 36 | tf_op jit(solution)/shard_map/ppermute | solution.py:127
  172.9 6.2 %collective-permute-start.7 = (f32[]{:T(128)}, f32[]{:T(128)}, u32[]{:S(2)}, u32[]{:S(2)}) collective-permute-start(f32[]{:T(128)} %add.95), channel_id=1, source_target_pairs={{0,32},{8,40},{16,48},{24,56},{32,0},{40,8},{48,16},{56,24},{1,33}... | collective-permute-start | bytes 20 | tf_op jit(solution)/shard_map/ppermute | solution.py:127
  179.1 3.1 %collective-permute-done.7 = f32[]{:T(128)} collective-permute-done((f32[]{:T(128)}, f32[]{:T(128)}, u32[]{:S(2)}, u32[]{:S(2)}) %collective-permute-start.7) | collective-permute-done | bytes 36 | tf_op jit(solution)/shard_map/ppermute | solution.py:127
  182.8 4.7 %collective-permute-start.8 = (f32[]{:T(128)}, f32[]{:T(128)}, u32[]{:S(2)}, u32[]{:S(2)}) collective-permute-start(f32[]{:T(128)} %add.96), channel_id=1, source_target_pairs={{0,64},{64,0},{128,192},{192,128},{256,320},{320,256},{384,448},{4... | collective-permute-start | bytes 20 | tf_op jit(solution)/shard_map/ppermute | solution.py:127
  188.9 6.2 %collective-permute-start.9 = (f32[]{:T(128)}, f32[]{:T(128)}, u32[]{:S(2)}, u32[]{:S(2)}) collective-permute-start(f32[]{:T(128)} %add.97), channel_id=1, source_target_pairs={{0,128},{64,192},{128,0},{192,64},{256,384},{320,448},{384,256},{4... | collective-permute-start | bytes 20 | tf_op jit(solution)/shard_map/ppermute | solution.py:127
  196.4 3.4 %collective-permute-start.10 = (f32[]{:T(128)}, f32[]{:T(128)}, u32[]{:S(2)}, u32[]{:S(2)}) collective-permute-start(f32[]{:T(128)} %add.98), channel_id=1, source_target_pairs={{0,256},{64,320},{128,384},{192,448},{256,0},{320,64},{384,128},{4... | collective-permute-start | bytes 20 | tf_op jit(solution)/shard_map/ppermute | solution.py:127
  199.8 6.0 %collective-permute-done.10 = f32[]{:T(128)} collective-permute-done((f32[]{:T(128)}, f32[]{:T(128)}, u32[]{:S(2)}, u32[]{:S(2)}) %collective-permute-start.10) | collective-permute-done | bytes 36 | tf_op jit(solution)/shard_map/ppermute | solution.py:127
  (71 shorter events, 37.3 us)
Async XLA Ops:
  0.6 13.3 %copy-start.4 = (bf16[128,512]{1,0:T(8,128)(2,1)S(1)}, bf16[128,512]{1,0:T(8,128)(2,1)}, u32[]{:S(2)}) copy-start(bf16[128,512]{1,0:T(8,128)(2,1)} %param.10) | copy-start | bytes 393220
  0.6 21.1 %copy-start.5 = (bf16[128,512]{1,0:T(8,128)(2,1)S(1)}, bf16[128,512]{1,0:T(8,128)(2,1)}, u32[]{:S(2)}) copy-start(bf16[128,512]{1,0:T(8,128)(2,1)} %param.7) | copy-start | bytes 393220
  3.5 72.5 %copy-start.3 = (bf16[512,512]{1,0:T(8,128)(2,1)S(1)}, bf16[512,512]{1,0:T(8,128)(2,1)}, u32[]{:S(2)}) copy-start(bf16[512,512]{1,0:T(8,128)(2,1)} %param.12) | copy-start | bytes 1572868
  3.5 73.4 %copy-start.6 = (bf16[128,512]{1,0:T(8,128)(2,1)S(1)}, bf16[128,512]{1,0:T(8,128)(2,1)}, u32[]{:S(2)}) copy-start(bf16[128,512]{1,0:T(8,128)(2,1)} %param.13) | copy-start | bytes 393220
  3.5 61.6 %all-to-all-start = ((bf16[8,128,1024]{1,2,0:T(8,128)(2,1)}), bf16[8,128,1024]{1,2,0:T(8,128)(2,1)S(1)}, u32[]{:S(2)}, u32[]{:S(2)}) async-start(bf16[8,128,1024]{1,2,0:T(8,128)(2,1)} %broadcast_in_dim.29), calls=%async_computation | async-start | bytes 4194304 | tf_op jit(solution)/shard_map/all_to_all | solution.py:21
  14.0 68.7 %collective-permute-start = (bf16[63,512]{1,0:T(8,128)(2,1)S(1)}, bf16[63,512]{1,0:T(8,128)(2,1)}, u32[]{:S(2)}, u32[]{:S(2)}) collective-permute-start(bf16[63,512]{1,0:T(8,128)(2,1)S(1)} %slice.37), channel_id=1, source_target_pairs={{8,0},{16,8},{24,16},{32,24},{40,32},{48,40},{56,48},{64,56},{72,6... | collective-permute-start | bytes 193544 | tf_op jit(solution)/shard_map/ppermute | solution.py:16
  66.3 33.2 %all-to-all-start.1 = ((bf16[8,128,512]{1,2,0:T(8,128)(2,1)}), bf16[8,128,512]{1,2,0:T(8,128)(2,1)}, u32[]{:S(2)}, u32[]{:S(2)}) async-start(bf16[8,128,512]{1,2,0:T(8,128)(2,1)} %broadcast_in_dim.52), calls=%async_computation.1 | async-start | bytes 2097152 | tf_op jit(solution)/shard_map/all_to_all | solution.py:21
  86.4 0.8 copy-start.1
  113.3 10.9 %copy-start.2 = (bf16[2,256,4,128]{3,2,1,0:T(4,128)(2,1)S(1)}, bf16[2,256,4,128]{3,2,1,0:T(4,128)(2,1)}, u32[]{:S(2)}) copy-start(bf16[2,256,4,128]{3,2,1,0:T(4,128)(2,1)} %reshape.103) | copy-start | bytes 1572868
  113.4 15.7 %copy-start = (bf16[2,256,4,128]{3,2,1,0:T(4,128)(2,1)S(1)}, bf16[2,256,4,128]{3,2,1,0:T(4,128)(2,1)}, u32[]{:S(2)}) copy-start(bf16[2,256,4,128]{3,2,1,0:T(4,128)(2,1)} %reshape.104) | copy-start | bytes 1572868
  114.5 95.5 %all-to-all-start.2 = ((bf16[8,128,524]{1,2,0:T(8,128)(2,1)}), bf16[8,128,524]{1,2,0:T(8,128)(2,1)S(1)}, u32[]{:S(2)}, u32[]{:S(2)}) async-start(bf16[8,128,524]{1,2,0:T(8,128)(2,1)} %pad_maximum_fusion), calls=%async_computation.2 | async-start | bytes 2162688 | tf_op jit(solution)/shard_map/all_to_all | solution.py:63
  132.1 76.4 %collective-permute-start.1 = (bf16[63,512]{1,0:T(8,128)(2,1)}, bf16[63,512]{1,0:T(8,128)(2,1)}, u32[]{:S(2)}, u32[]{:S(2)}) collective-permute-start(bf16[63,512]{1,0:T(8,128)(2,1)} %slice.46), channel_id=1, source_target_pairs={{0,8},{8,16},{16,24},{24,32},{32,40},{40,48},{48,56},{56,64},{64,7... | collective-permute-start | bytes 193544 | tf_op jit(solution)/shard_map/ppermute | solution.py:16
  143.3 3.0 %collective-permute-start.2 = (f32[]{:T(128)}, f32[]{:T(128)}, u32[]{:S(2)}, u32[]{:S(2)}) collective-permute-start(f32[]{:T(128)} %add.90), channel_id=1, source_target_pairs={{0,1},{1,0},{2,3},{3,2},{4,5},{5,4},{6,7},{7,6},{8,9},{9,8},{10,11... | collective-permute-start | bytes 20 | tf_op jit(solution)/shard_map/ppermute | solution.py:127
  146.9 5.4 %collective-permute-start.3 = (f32[]{:T(128)}, f32[]{:T(128)}, u32[]{:S(2)}, u32[]{:S(2)}) collective-permute-start(f32[]{:T(128)} %add.91), channel_id=1, source_target_pairs={{0,2},{1,3},{2,0},{3,1},{4,6},{5,7},{6,4},{7,5},{8,10},{9,11},{10,... | collective-permute-start | bytes 20 | tf_op jit(solution)/shard_map/ppermute | solution.py:127
  153.0 6.3 %collective-permute-start.4 = (f32[]{:T(128)}, f32[]{:T(128)}, u32[]{:S(2)}, u32[]{:S(2)}) collective-permute-start(f32[]{:T(128)} %add.92), channel_id=1, source_target_pairs={{0,4},{1,5},{2,6},{3,7},{4,0},{5,1},{6,2},{7,3},{8,12},{9,13},{10,... | collective-permute-start | bytes 20 | tf_op jit(solution)/shard_map/ppermute | solution.py:127
  159.9 5.4 %collective-permute-start.5 = (f32[]{:T(128)}, f32[]{:T(128)}, u32[]{:S(2)}, u32[]{:S(2)}) collective-permute-start(f32[]{:T(128)} %add.93), channel_id=1, source_target_pairs={{0,8},{8,0},{16,24},{24,16},{32,40},{40,32},{48,56},{56,48},{1,9},... | collective-permute-start | bytes 20 | tf_op jit(solution)/shard_map/ppermute | solution.py:127
  166.0 6.3 %collective-permute-start.6 = (f32[]{:T(128)}, f32[]{:T(128)}, u32[]{:S(2)}, u32[]{:S(2)}) collective-permute-start(f32[]{:T(128)} %add.94), channel_id=1, source_target_pairs={{0,16},{8,24},{16,0},{24,8},{32,48},{40,56},{48,32},{56,40},{1,17}... | collective-permute-start | bytes 20 | tf_op jit(solution)/shard_map/ppermute | solution.py:127
  172.9 9.3 %collective-permute-start.7 = (f32[]{:T(128)}, f32[]{:T(128)}, u32[]{:S(2)}, u32[]{:S(2)}) collective-permute-start(f32[]{:T(128)} %add.95), channel_id=1, source_target_pairs={{0,32},{8,40},{16,48},{24,56},{32,0},{40,8},{48,16},{56,24},{1,33}... | collective-permute-start | bytes 20 | tf_op jit(solution)/shard_map/ppermute | solution.py:127
  182.8 5.4 %collective-permute-start.8 = (f32[]{:T(128)}, f32[]{:T(128)}, u32[]{:S(2)}, u32[]{:S(2)}) collective-permute-start(f32[]{:T(128)} %add.96), channel_id=1, source_target_pairs={{0,64},{64,0},{128,192},{192,128},{256,320},{320,256},{384,448},{4... | collective-permute-start | bytes 20 | tf_op jit(solution)/shard_map/ppermute | solution.py:127
  188.9 6.9 %collective-permute-start.9 = (f32[]{:T(128)}, f32[]{:T(128)}, u32[]{:S(2)}, u32[]{:S(2)}) collective-permute-start(f32[]{:T(128)} %add.97), channel_id=1, source_target_pairs={{0,128},{64,192},{128,0},{192,64},{256,384},{320,448},{384,256},{4... | collective-permute-start | bytes 20 | tf_op jit(solution)/shard_map/ppermute | solution.py:127
  196.4 9.3 %collective-permute-start.10 = (f32[]{:T(128)}, f32[]{:T(128)}, u32[]{:S(2)}, u32[]{:S(2)}) collective-permute-start(f32[]{:T(128)} %add.98), channel_id=1, source_target_pairs={{0,256},{64,320},{128,384},{192,448},{256,0},{320,64},{384,128},{4... | collective-permute-start | bytes 20 | tf_op jit(solution)/shard_map/ppermute | solution.py:127

commit v5 on v3

--- a/solution.py
+++ b/solution.py
@@ -5,6 +5,7 @@
 from jax import lax
 from jax.sharding import Mesh
 from jax.sharding import PartitionSpec as P
+
 
 HD = 128
 SPAN = 64
@@ -27,13 +28,15 @@
     outer_index = lax.axis_index("outer")
     z_index = lax.axis_index("z")
     pair = jnp.concatenate([k_self, v_self], axis=1)
-    group = spread(pair, "z", z_count).reshape(z_count * row_count, 2 * column_count)
-    keys = group[:, :column_count].reshape(z_count * row_count, head_count, HD)
-    values = group[:, column_count:].reshape(z_count * row_count, head_count, HD)
-    queries = spread(q_self, "outer", outer_count).reshape(outer_count, row_count, head_count, HD)
-    key_first = outer_index * z_count * row_count
-    key_positions = key_first + jnp.arange(z_count * row_count, dtype=jnp.int32)
-    query_starts = (jnp.arange(outer_count, dtype=jnp.int32) * z_count + z_index) * row_count
+    group = spread(pair, "outer", outer_count).reshape(outer_count * row_count, 2 * column_count)
+    keys = group[:, :column_count].reshape(outer_count * row_count, head_count, HD)
+    values = group[:, column_count:].reshape(outer_count * row_count, head_count, HD)
+    queries = spread(q_self, "z", z_count).reshape(z_count, row_count, head_count, HD)
+    key_starts = (jnp.arange(outer_count, dtype=jnp.int32) * z_count + z_index) * row_count
+    key_positions = (
+        key_starts[:, None] + jnp.arange(row_count, dtype=jnp.int32)[None, :]
+    ).reshape(outer_count * row_count)
+    query_starts = (outer_index * z_count + jnp.arange(z_count, dtype=jnp.int32)) * row_count
     query_positions = query_starts[:, None] + jnp.arange(row_count, dtype=jnp.int32)[None, :]
     visible = (key_positions[None, None, :] <= query_positions[:, :, None])[None]
     scores = jnp.einsum("grhd,khd->hgrk", queries, keys, preferred_element_type=jnp.float32) * (
@@ -53,15 +56,15 @@
     level = level.transpose(1, 2, 0)
     pieces = []
     rest = level
-    for unused in range(3):
+    for _ in range(3):
         piece = lax.optimization_barrier(rest.astype(jnp.bfloat16))
         pieces.append(piece)
         rest = rest - piece.astype(jnp.float32)
     packed = jnp.concatenate(
-        [part_out.reshape(outer_count, row_count, column_count)] + pieces, axis=2
+        [part_out.reshape(z_count, row_count, column_count)] + pieces, axis=2
     )
-    back = lax.all_to_all(packed, "outer", 0, 0, tiled=True)
-    got_out = back[:, :, :column_count].reshape(outer_count, row_count, head_count, HD)
+    back = lax.all_to_all(packed, "z", 0, 0, tiled=True)
+    got_out = back[:, :, :column_count].reshape(z_count, row_count, head_count, HD)
     got_level = sum(
         back[:, :, column_count + i * head_count : column_count + (i + 1) * head_count].astype(
             jnp.float32

time: 176 us -> 170 us (0.966)
  the two profiles are of different devices: /device:TPU:40 before, /device:TPU:1 now
where the time goes in v5:
time: 170 us; the launch traced here: 169 us
  starting transfers between devices  59.7 us (35%)
  waiting for transfers between devices  49.4 us (29%)
  matrix products  29.6 us (17%)
  local copies, waits for them, and re-layouts  14 us (8%)
  other arithmetic  13.4 us (8%)
  between operations  2.97 us (2%)
    all_to_all x2, waiting for transfers between devices, spread(): return lax.all_to_all(copies, axis, 0, 0, tiled=True)  37.8 us
    all_to_all x1, starting transfers between devices, cross_attention(): lax.all_to_all(jnp.broadcast_to(squares[None], (device_count,)), ('outer'...  26.5 us
    all_to_all x2, starting transfers between devices, spread(): return lax.all_to_all(copies, axis, 0, 0, tiled=True)  21 us
    all_to_all x1, starting transfers between devices, self_attention(): back = lax.all_to_all(packed, 'z', 0, 0, tiled=True)  6.97 us
    all_to_all x1, waiting for transfers between devices, self_attention(): back = lax.all_to_all(packed, 'z', 0, 0, tiled=True)  5.93 us
    dot_general x1, matrix products, cross_attention(): jnp.einsum('chrk,crhd->ckhd', grad_scores, queries, preferred_element_typ...  5.69 us
    ppermute x2, starting transfers between devices, from_behind(): return lax.ppermute(block, CTX, route)  5.25 us
    dot_general x1, matrix products, self_attention(): jnp.einsum('hgrk,khd->grhd', weights.astype(jnp.bfloat16), values, prefer...  4.99 us
  transfers between devices with their start and end apart: 6, of which 5 were waited for; matrix products, arithmetic and copies ran while one was open for 30% of the time, Pallas kernels for 0%

profile of v5, /device:TPU:1, one launch (start us, length us, event | category | flops | bytes accessed | tf_op | source)
XLA Modules:
  0.0 169.1 jit_solution(10680531349457229917)
XLA Ops:
  1.9 1.6 broadcast_in_dim.31
  3.5 10.1 %all-to-all-start = ((bf16[8,128,1024]{1,2,0:T(8,128)(2,1)}), bf16[8,128,1024]{1,2,0:T(8,128)(2,1)S(1)}, u32[]{:S(2)}, u32[]{:S(2)}) async-start(bf16[8,128,1024]{1,2,0:T(8,128)(2,1)} %broadcast_in_dim.31), calls=%async_computation | async-start | bytes 4194304 | tf_op jit(solution)/shard_map/all_to_all | solution.py:22
  14.3 1.3 collective-permute-start
  17.5 37.3 %all-to-all-done = bf16[8,128,1024]{1,2,0:T(8,128)(2,1)S(1)} async-done(((bf16[8,128,1024]{1,2,0:T(8,128)(2,1)}), bf16[8,128,1024]{1,2,0:T(8,128)(2,1)S(1)}, u32[]{:S(2)}, u32[]{:S(2)}) %all-to-all-start) | async-done | bytes 2097184 | tf_op jit(solution)/shard_map/all_to_all | solution.py:22
  56.0 10.9 %all-to-all-start.1 = ((bf16[8,128,512]{1,2,0:T(8,128)(2,1)}), bf16[8,128,512]{1,2,0:T(8,128)(2,1)}, u32[]{:S(2)}, u32[]{:S(2)}) async-start(bf16[8,128,512]{1,2,0:T(8,128)(2,1)} %broadcast_in_dim.33), calls=%async_computation.1 | async-start | bytes 2097152 | tf_op jit(solution)/shard_map/all_to_all | solution.py:22
  66.9 2.1 %fusion.29 = f32[2,4,64,256]{3,2,1,0:T(8,128)} fusion(bf16[2,256,4,128]{3,2,1,0:T(4,128)(2,1)} %reshape.122, bf16[2,64,4,128]{3,2,1,0:T(4,128)(2,1)S(1)} %reshape.123), kind=kOutput, calls=%fused_computation.41 | convolution fusion | flops 33554432 | bytes 1179648 | tf_op jit(solution)/shard_map/crhd,ckhd->chrk/dot_general | solution.py:107
  69.0 2.0 %reshape.121 = bf16[2,256,4,128]{3,2,1,0:T(4,128)(2,1)} reshape(bf16[512,512]{1,0:T(8,128)(2,1)} %param.11) | data formatting | bytes 1048576 | tf_op jit(solution)/shard_map/reshape | solution.py:92
  71.9 1.3 convolution_multiply_fusion
  75.0 4.1 %multiply_reduce_fusion = (f32[]{:T(128)}, f32[2,4,256,128]{3,2,1,0:T(8,128)}) fusion(bf16[2,64,4,128]{3,2,1,0:T(4,128)(2,1)S(1)} %reshape.123, f32[2,4,64]{2,1,0:T(4,128)S(1)} %get-tuple-element.28, f32[2,4,64,256]{3,2,1,0:T(8,128)} %copy-done.1), kind=kOutput, calls=%fused_computation.32 | convolution fusion | flops 34472704 | bytes 1705988 | tf_op jit(solution)/shard_map/chrk,crhd->ckhd/dot_general | solution.py:119
  79.1 5.7 %multiply_reduce_fusion.1 = (f32[]{:T(128)}, f32[2,4,128,256]{3,2,1,0:T(8,128)}) fusion(f32[2,4,64,256]{3,2,1,0:T(8,128)} %fusion.29, f32[2,4,64,256]{3,2,1,0:T(8,128)} %get-tuple-element.29, f32[2,4,64]{2,1,0:T(4,128)S(1)} %get-tuple-element.28, bf16[2,64,4,128]{3,2,1,0:T(4,128)(2,1)S(1)} %reshape.120), kind=kOutput, calls=%fused_computation.33 | convolution fusion | flops 34996992 | bytes 2230276 | tf_op jit(solution)/shard_map/chrk,crhd->ckhd/dot_general | solution.py:116
  87.9 26.5 %all-to-all-start.3 = ((f32[512,1,1]{2,1,0:T(1,128)}), f32[512,1,1]{2,1,0:T(1,128)S(1)}, u32[]{:S(2)}, u32[]{:S(2)}) async-start(f32[512,1,1]{2,1,0:T(1,128)} %broadcast_in_dim.63), calls=%async_computation.3 | async-start | bytes 524288 | tf_op jit(solution)/shard_map/all_to_all | solution.py:126
  114.4 4.5 %fusion.2 = (f32[4,8,128]{2,1,0:T(8,128)S(1)}, f32[4,1024,8,128]{3,1,2,0:T(8,128)S(1)}) fusion(pred[8,128,1024]{1,2,0:T(8,128)(4,1)S(1)} %broadcast_compare_fusion, bf16[1024,4,128,1]{0,2,3,1:T(8,128)(2,1)S(1)} %bitcast.106, bf16[8,128,4,128]{1,3,2,0:T(8,128)(2,1)} %bitcast.6), kind=kOutput, calls=%fused_computation.4 | convolution fusion | flops 1086320640 | bytes 19939328 | tf_op jit(solution)/shard_map/grhd,khd->hgrk/dot_general | solution.py:42
  119.0 4.2 %fusion.3 = f32[4,8,128]{2,1,0:T(8,128)S(1)} fusion(f32[4,1024,8,128]{3,1,2,0:T(8,128)S(1)} %get-tuple-element.27, f32[4,8,128]{2,1,0:T(8,128)S(1)} %get-tuple-element.26, pred[8,128,1024]{1,2,0:T(8,128)(4,1)S(1)} %broadcast_compare_fusion), kind=kLoop, calls=%fused_computation.5 | loop fusion | flops 20967424 | bytes 17858560 | tf_op jit(solution)/shard_map/reduce_sum | solution.py:48
  123.3 5.0 %fusion.9 = bf16[8,128,4,128]{1,3,0,2:T(8,128)(2,1)S(1)} fusion(bf16[1024,4,128,1]{0,2,3,1:T(8,128)(2,1)S(1)} %bitcast.105, f32[4,1024,8,128]{3,1,2,0:T(8,128)S(1)} %get-tuple-element.27, f32[4,8,128]{2,1,0:T(8,128)S(1)} %get-tuple-element.26, pred[8,128,1024]{1,2,0:T(8,128)(4,1)S(1)} %broadcast_compare_fusion, f32[8,128,4]{1,0,2:T(8,128)S(1)} %get-tuple-element.24), kind=kOutput, calls=%fused_computation.13 | convolution fusion | flops 1095761920 | bytes 19955712 | tf_op jit(solution)/shard_map/hgrk,khd->grhd/dot_general | solution.py:49
  129.5 1.6 all-to-all-done.3
  131.0 7.0 %all-to-all-start.2 = ((bf16[8,128,524]{1,2,0:T(8,128)(2,1)}), bf16[8,128,524]{1,2,0:T(8,128)(2,1)S(1)}, u32[]{:S(2)}, u32[]{:S(2)}) async-start(bf16[8,128,524]{1,2,0:T(8,128)(2,1)} %pad_maximum_fusion), calls=%async_computation.2 | async-start | bytes 2162688 | tf_op jit(solution)/shard_map/all_to_all | solution.py:66
  138.0 4.7 %fusion.19 = bf16[2,64,4,128]{3,1,2,0:T(8,128)(2,1)} fusion(f32[2,4,64,256]{3,2,1,0:T(8,128)} %fusion.29, bf16[2,256,4,128]{3,2,1,0:T(4,128)(2,1)S(1)} %copy-done.2, f32[2,4,64,256]{3,2,1,0:T(8,128)} %get-tuple-element.29, f32[2,4,64]{2,1,0:T(4,128)S(1)} %get-tuple-element.28), kind=kOutput, calls=%fused_computation.25 | convolution fusion | flops 34538240 | bytes 1705984 | tf_op jit(solution)/shard_map/chrk,ckhd->crhd/dot_general | solution.py:112
  144.5 4.0 %collective-permute-start.1 = (bf16[63,512]{1,0:T(8,128)(2,1)}, bf16[63,512]{1,0:T(8,128)(2,1)}, u32[]{:S(2)}, u32[]{:S(2)}) collective-permute-start(bf16[63,512]{1,0:T(8,128)(2,1)} %slice.46), channel_id=1, source_target_pairs={{0,8},{8,16},{16,24},{24,32},{32,40},{40,48},{48,56},{56,64},{64,7... | collective-permute-start | bytes 193544 | tf_op jit(solution)/shard_map/ppermute | solution.py:17
  148.5 2.2 %fusion.18 = bf16[2,64,4,128]{3,1,2,0:T(8,128)(2,1)S(1)} fusion(bf16[2,256,4,128]{3,2,1,0:T(4,128)(2,1)S(1)} %copy-done, f32[2,4,64]{2,1,0:T(4,128)S(1)} %get-tuple-element.28, f32[2,4,64,256]{3,2,1,0:T(8,128)} %copy-done.1), kind=kOutput, calls=%fused_computation.24 | convolution fusion | flops 34013952 | bytes 1181696 | tf_op jit(solution)/shard_map/chrk,ckhd->crhd/dot_general | solution.py:103
  151.5 1.1 reduce_sum.82
  153.3 1.3 fusion.27
  156.5 4.0 %collective-permute-done.1 = bf16[63,512]{1,0:T(8,128)(2,1)} collective-permute-done((bf16[63,512]{1,0:T(8,128)(2,1)}, bf16[63,512]{1,0:T(8,128)(2,1)}, u32[]{:S(2)}, u32[]{:S(2)}) %collective-permute-start.1) | collective-permute-done | bytes 64544 | tf_op jit(solution)/shard_map/ppermute | solution.py:17
  160.6 1.5 pad_maximum_fusion.3
  162.1 5.9 %all-to-all-done.2 = bf16[8,128,524]{1,2,0:T(8,128)(2,1)S(1)} async-done(((bf16[8,128,524]{1,2,0:T(8,128)(2,1)}), bf16[8,128,524]{1,2,0:T(8,128)(2,1)S(1)}, u32[]{:S(2)}, u32[]{:S(2)}) %all-to-all-start.2) | async-done | bytes 1073184 | tf_op jit(solution)/shard_map/all_to_all | solution.py:66
  (60 shorter events, 16.1 us)
Async XLA Ops:
  0.6 13.0 %copy-start.5 = (bf16[128,512]{1,0:T(8,128)(2,1)S(1)}, bf16[128,512]{1,0:T(8,128)(2,1)}, u32[]{:S(2)}) copy-start(bf16[128,512]{1,0:T(8,128)(2,1)} %param.10) | copy-start | bytes 393220
  0.6 14.9 %copy-start.6 = (bf16[128,512]{1,0:T(8,128)(2,1)S(1)}, bf16[128,512]{1,0:T(8,128)(2,1)}, u32[]{:S(2)}) copy-start(bf16[128,512]{1,0:T(8,128)(2,1)} %param.7) | copy-start | bytes 393220
  0.7 15.1 %copy-start.4 = (bf16[512,512]{1,0:T(8,128)(2,1)S(1)}, bf16[512,512]{1,0:T(8,128)(2,1)}, u32[]{:S(2)}) copy-start(bf16[512,512]{1,0:T(8,128)(2,1)} %param.12) | copy-start | bytes 1572868
  1.9 14.7 %copy-start.7 = (bf16[128,512]{1,0:T(8,128)(2,1)S(1)}, bf16[128,512]{1,0:T(8,128)(2,1)}, u32[]{:S(2)}) copy-start(bf16[128,512]{1,0:T(8,128)(2,1)} %param.13) | copy-start | bytes 393220
  3.5 51.3 %all-to-all-start = ((bf16[8,128,1024]{1,2,0:T(8,128)(2,1)}), bf16[8,128,1024]{1,2,0:T(8,128)(2,1)S(1)}, u32[]{:S(2)}, u32[]{:S(2)}) async-start(bf16[8,128,1024]{1,2,0:T(8,128)(2,1)} %broadcast_in_dim.31), calls=%async_computation | async-start | bytes 4194304 | tf_op jit(solution)/shard_map/all_to_all | solution.py:22
  14.3 56.7 %collective-permute-start = (bf16[63,512]{1,0:T(8,128)(2,1)}, bf16[63,512]{1,0:T(8,128)(2,1)}, u32[]{:S(2)}, u32[]{:S(2)}) collective-permute-start(bf16[63,512]{1,0:T(8,128)(2,1)} %slice.37), channel_id=1, source_target_pairs={{8,0},{16,8},{24,16},{32,24},{40,32},{48,40},{56,48},{64,56},{72,6... | collective-permute-start | bytes 193544 | tf_op jit(solution)/shard_map/ppermute | solution.py:17
  56.0 31.1 %all-to-all-start.1 = ((bf16[8,128,512]{1,2,0:T(8,128)(2,1)}), bf16[8,128,512]{1,2,0:T(8,128)(2,1)}, u32[]{:S(2)}, u32[]{:S(2)}) async-start(bf16[8,128,512]{1,2,0:T(8,128)(2,1)} %broadcast_in_dim.33), calls=%async_computation.1 | async-start | bytes 2097152 | tf_op jit(solution)/shard_map/all_to_all | solution.py:22
  73.3 0.8 copy-start.1
  87.9 43.2 %all-to-all-start.3 = ((f32[512,1,1]{2,1,0:T(1,128)}), f32[512,1,1]{2,1,0:T(1,128)S(1)}, u32[]{:S(2)}, u32[]{:S(2)}) async-start(f32[512,1,1]{2,1,0:T(1,128)} %broadcast_in_dim.63), calls=%async_computation.3 | async-start | bytes 524288 | tf_op jit(solution)/shard_map/all_to_all | solution.py:126
  128.3 9.8 %copy-start.2 = (bf16[2,256,4,128]{3,2,1,0:T(4,128)(2,1)S(1)}, bf16[2,256,4,128]{3,2,1,0:T(4,128)(2,1)}, u32[]{:S(2)}) copy-start(bf16[2,256,4,128]{3,2,1,0:T(4,128)(2,1)} %reshape.121) | copy-start | bytes 1572868
  128.4 20.1 %copy-start = (bf16[2,256,4,128]{3,2,1,0:T(4,128)(2,1)S(1)}, bf16[2,256,4,128]{3,2,1,0:T(4,128)(2,1)}, u32[]{:S(2)}) copy-start(bf16[2,256,4,128]{3,2,1,0:T(4,128)(2,1)} %reshape.122) | copy-start | bytes 1572868
  131.0 37.0 %all-to-all-start.2 = ((bf16[8,128,524]{1,2,0:T(8,128)(2,1)}), bf16[8,128,524]{1,2,0:T(8,128)(2,1)S(1)}, u32[]{:S(2)}, u32[]{:S(2)}) async-start(bf16[8,128,524]{1,2,0:T(8,128)(2,1)} %pad_maximum_fusion), calls=%async_computation.2 | async-start | bytes 2162688 | tf_op jit(solution)/shard_map/all_to_all | solution.py:66
  142.7 12.1 %copy-start.3 = (f32[2,4,256,128]{3,2,1,0:T(8,128)S(1)}, f32[2,4,256,128]{3,2,1,0:T(8,128)}, u32[]{:S(2)}) copy-start(f32[2,4,256,128]{3,2,1,0:T(8,128)} %get-tuple-element.33) | copy-start | bytes 3145732
  144.5 16.0 %collective-permute-start.1 = (bf16[63,512]{1,0:T(8,128)(2,1)}, bf16[63,512]{1,0:T(8,128)(2,1)}, u32[]{:S(2)}, u32[]{:S(2)}) collective-permute-start(bf16[63,512]{1,0:T(8,128)(2,1)} %slice.46), channel_id=1, source_target_pairs={{0,8},{8,16},{16,24},{24,32},{32,40},{40,48},{48,56},{56,64},{64,7... | collective-permute-start | bytes 193544 | tf_op jit(solution)/shard_map/ppermute | solution.py:17

commit v6 on v3

--- a/solution.py
+++ b/solution.py
@@ -5,6 +5,7 @@
 from jax import lax
 from jax.sharding import Mesh
 from jax.sharding import PartitionSpec as P
+
 
 HD = 128
 SPAN = 64
@@ -53,19 +54,19 @@
     level = level.transpose(1, 2, 0)
     pieces = []
     rest = level
-    for unused in range(3):
+    for _ in range(3):
         piece = lax.optimization_barrier(rest.astype(jnp.bfloat16))
         pieces.append(piece)
         rest = rest - piece.astype(jnp.float32)
+    stat_rows = jnp.concatenate(pieces, axis=2).reshape(outer_count, -1, column_count)
     packed = jnp.concatenate(
-        [part_out.reshape(outer_count, row_count, column_count)] + pieces, axis=2
+        [part_out.reshape(outer_count, row_count, column_count), stat_rows], axis=1
     )
     back = lax.all_to_all(packed, "outer", 0, 0, tiled=True)
-    got_out = back[:, :, :column_count].reshape(outer_count, row_count, head_count, HD)
+    got_out = back[:, :row_count].reshape(outer_count, row_count, head_count, HD)
+    got_stats = back[:, row_count:].reshape(outer_count, row_count, 3 * head_count)
     got_level = sum(
-        back[:, :, column_count + i * head_count : column_count + (i + 1) * head_count].astype(
-            jnp.float32
-        )
+        got_stats[:, :, i * head_count : (i + 1) * head_count].astype(jnp.float32)
         for i in range(3)
     )
     top = jnp.max(got_level, axis=0)

time: 176 us -> 190 us (1.080)
  local copies, waits for them, and re-layouts: 14 us -> 22 us
  matrix products: 29.6 us -> 32.8 us
    dot_general x1, matrix products: 4.99 us -> 8.73 us  [self_attention(): jnp.einsum('hgrk,khd->grhd', weights.astype(jnp.bfloat16), values, prefer...]
    mul x0 -> x2, local copies, waits for them, and re-layouts: none -> 3.15 us  [self_attention(): mixed = jnp.sum(got_out.astype(jnp.float32) * rescale[..., None], axis=0)]
    concatenate x0 -> x2, local copies, waits for them, and re-layouts: none -> 2.29 us  [the longest x1 2.09 us: self_attention(): jnp.concatenate([part_out.reshape(outer_count, row_count, column_count),...]
    unnamed x20 -> x21, local copies, waits for them, and re-layouts: 2.41 us -> 4.01 us
  transfers between devices with their start and end apart: 6 -> 6, of which waited for: 3 -> 3; matrix products, arithmetic and copies ran while one was open for 29% -> 30% of each run, Pallas kernels for 0% -> 0%
where the time goes in v6:
time: 190 us; the launch traced here: 189 us
  waiting for transfers between devices  61.9 us (33%)
  starting transfers between devices  54.2 us (29%)
  matrix products  32.8 us (17%)
  local copies, waits for them, and re-layouts  22 us (12%)
  other arithmetic  15.2 us (8%)
  between operations  3.02 us (2%)
    all_to_all x2, waiting for transfers between devices, spread(): return lax.all_to_all(copies, axis, 0, 0, tiled=True)  43.7 us
    all_to_all x2, starting transfers between devices, spread(): return lax.all_to_all(copies, axis, 0, 0, tiled=True)  20 us
    ppermute x2, waiting for transfers between devices, from_behind(): return lax.ppermute(block, CTX, route)  18.2 us
    all_to_all x1, starting transfers between devices, cross_attention(): lax.all_to_all(jnp.broadcast_to(squares[None], (device_count,)), ('outer'...  12.7 us
    ppermute x2, starting transfers between devices, from_behind(): return lax.ppermute(block, CTX, route)  11.9 us
    all_to_all x1, starting transfers between devices, self_attention(): back = lax.all_to_all(packed, 'outer', 0, 0, tiled=True)  9.64 us
    dot_general x1, matrix products, self_attention(): jnp.einsum('hgrk,khd->grhd', weights.astype(jnp.bfloat16), values, prefer...  8.73 us
    dot_general x1, matrix products, cross_attention(): jnp.einsum('chrk,crhd->ckhd', grad_scores, queries, preferred_element_typ...  5.72 us
  transfers between devices with their start and end apart: 6, of which 3 were waited for; matrix products, arithmetic and copies ran while one was open for 30% of the time, Pallas kernels for 0%

profile of v6, /device:TPU:40, one launch (start us, length us, event | category | flops | bytes accessed | tf_op | source)
XLA Modules:
  0.0 189.2 jit_solution(4704025803710950417)
XLA Ops:
  1.9 1.6 broadcast_in_dim.31
  3.5 10.3 %all-to-all-start = ((bf16[8,128,1024]{1,2,0:T(8,128)(2,1)}), bf16[8,128,1024]{1,2,0:T(8,128)(2,1)S(1)}, u32[]{:S(2)}, u32[]{:S(2)}) async-start(bf16[8,128,1024]{1,2,0:T(8,128)(2,1)} %broadcast_in_dim.31), calls=%async_computation | async-start | bytes 4194304 | tf_op jit(solution)/shard_map/all_to_all | solution.py:22
  14.5 7.8 %collective-permute-start = (bf16[63,512]{1,0:T(8,128)(2,1)}, bf16[63,512]{1,0:T(8,128)(2,1)}, u32[]{:S(2)}, u32[]{:S(2)}) collective-permute-start(bf16[63,512]{1,0:T(8,128)(2,1)} %slice.41), channel_id=1, source_target_pairs={{8,0},{16,8},{24,16},{32,24},{40,32},{48,40},{56,48},{64,56},{72,6... | collective-permute-start | bytes 193544 | tf_op jit(solution)/shard_map/ppermute | solution.py:17
  24.2 40.9 %all-to-all-done = bf16[8,128,1024]{1,2,0:T(8,128)(2,1)S(1)} async-done(((bf16[8,128,1024]{1,2,0:T(8,128)(2,1)}), bf16[8,128,1024]{1,2,0:T(8,128)(2,1)S(1)}, u32[]{:S(2)}, u32[]{:S(2)}) %all-to-all-start) | async-done | bytes 2097184 | tf_op jit(solution)/shard_map/all_to_all | solution.py:22
  66.2 9.7 %all-to-all-start.1 = ((bf16[8,128,512]{1,2,0:T(8,128)(2,1)}), bf16[8,128,512]{1,2,0:T(8,128)(2,1)}, u32[]{:S(2)}, u32[]{:S(2)}) async-start(bf16[8,128,512]{1,2,0:T(8,128)(2,1)} %broadcast_in_dim.33), calls=%async_computation.1 | async-start | bytes 2097152 | tf_op jit(solution)/shard_map/all_to_all | solution.py:22
  75.9 2.2 %fusion.28 = f32[2,4,64,256]{3,2,1,0:T(8,128)} fusion(bf16[2,256,4,128]{3,2,1,0:T(4,128)(2,1)} %reshape.115, bf16[2,64,4,128]{3,2,1,0:T(4,128)(2,1)S(1)} %reshape.116), kind=kOutput, calls=%fused_computation.42 | convolution fusion | flops 33554432 | bytes 1179648 | tf_op jit(solution)/shard_map/crhd,ckhd->chrk/dot_general | solution.py:105
  78.1 2.0 %reshape.114 = bf16[2,256,4,128]{3,2,1,0:T(4,128)(2,1)} reshape(bf16[512,512]{1,0:T(8,128)(2,1)} %param.11) | data formatting | bytes 1048576 | tf_op jit(solution)/shard_map/reshape | solution.py:90
  80.9 1.4 convolution_multiply_fusion
  84.0 4.1 %multiply_reduce_fusion.1 = (f32[]{:T(128)}, f32[2,4,256,128]{3,2,1,0:T(8,128)}) fusion(bf16[2,64,4,128]{3,2,1,0:T(4,128)(2,1)S(1)} %reshape.116, f32[2,4,64]{2,1,0:T(4,128)S(1)} %get-tuple-element.33, f32[2,4,64,256]{3,2,1,0:T(8,128)} %copy-done.2), kind=kOutput, calls=%fused_computation.31 | convolution fusion | flops 34472704 | bytes 1705988 | tf_op jit(solution)/shard_map/chrk,crhd->ckhd/dot_general | solution.py:117
  88.1 5.7 %multiply_reduce_fusion.2 = (f32[]{:T(128)}, f32[2,4,128,256]{3,2,1,0:T(8,128)}) fusion(f32[2,4,64,256]{3,2,1,0:T(8,128)} %fusion.28, f32[2,4,64,256]{3,2,1,0:T(8,128)} %get-tuple-element.34, f32[2,4,64]{2,1,0:T(4,128)S(1)} %get-tuple-element.33, bf16[2,64,4,128]{3,2,1,0:T(4,128)(2,1)S(1)} %reshape.113), kind=kOutput, calls=%fused_computation.32 | convolution fusion | flops 34996992 | bytes 2230276 | tf_op jit(solution)/shard_map/chrk,crhd->ckhd/dot_general | solution.py:114
  96.6 2.8 %all-to-all-done.1 = bf16[8,128,512]{1,2,0:T(8,128)(2,1)} async-done(((bf16[8,128,512]{1,2,0:T(8,128)(2,1)}), bf16[8,128,512]{1,2,0:T(8,128)(2,1)}, u32[]{:S(2)}, u32[]{:S(2)}) %all-to-all-start.1) | async-done | bytes 1048608 | tf_op jit(solution)/shard_map/all_to_all | solution.py:22
  100.3 12.7 %all-to-all-start.3 = ((f32[512,1,1]{2,1,0:T(1,128)}), f32[512,1,1]{2,1,0:T(1,128)S(1)}, u32[]{:S(2)}, u32[]{:S(2)}) async-start(f32[512,1,1]{2,1,0:T(1,128)} %broadcast_in_dim.62), calls=%async_computation.3 | async-start | bytes 524288 | tf_op jit(solution)/shard_map/all_to_all | solution.py:124
  113.0 4.5 %fusion.2 = (f32[4,8,128]{2,1,0:T(8,128)S(1)}, f32[4,1024,8,128]{3,1,2,0:T(8,128)S(1)}) fusion(pred[8,128,1024]{1,2,0:T(8,128)(4,1)S(1)} %broadcast_compare_fusion, bf16[1024,4,128,1]{0,2,3,1:T(8,128)(2,1)S(1)} %bitcast.100, bf16[8,128,4,128]{1,3,2,0:T(8,128)(2,1)} %bitcast.5), kind=kOutput, calls=%fused_computation.4 | convolution fusion | flops 1086320640 | bytes 19939328 | tf_op jit(solution)/shard_map/grhd,khd->hgrk/dot_general | solution.py:40
  117.5 4.2 %fusion.3 = f32[4,8,128]{2,1,0:T(8,128)S(1)} fusion(f32[4,1024,8,128]{3,1,2,0:T(8,128)S(1)} %get-tuple-element.32, f32[4,8,128]{2,1,0:T(8,128)S(1)} %get-tuple-element.31, pred[8,128,1024]{1,2,0:T(8,128)(4,1)S(1)} %broadcast_compare_fusion), kind=kLoop, calls=%fused_computation.5 | loop fusion | flops 20967424 | bytes 17858560 | tf_op jit(solution)/shard_map/reduce_sum | solution.py:46
  121.7 1.5 copy-done
  124.4 8.7 %fusion.8 = bf16[8,128,4,128]{1,3,0,2:T(8,128)(2,1)S(1)} fusion(bf16[1024,4,128,1]{0,2,3,1:T(8,128)(2,1)} %bitcast.99, f32[4,1024,8,128]{3,1,2,0:T(8,128)} %copy-done, f32[4,8,128]{2,1,0:T(8,128)S(1)} %get-tuple-element.31, pred[8,128,1024]{1,2,0:T(8,128)(4,1)S(1)} %broadcast_compare_fusion, f32[8,128,4]{1,0,2:T(8,128)S(1)} %get-tuple-element.29), kind=kOutput, calls=%fused_computation.12 | convolution fusion | flops 1095761920 | bytes 19955712 | tf_op jit(solution)/shard_map/hgrk,khd->grhd/dot_general | solution.py:47
  133.7 2.1 %copy.126 = bf16[8,131,512]{2,1,0:T(8,128)(2,1)} copy(bf16[8,131,512]{1,2,0:T(8,128)(2,1)S(1)} %pad_maximum_fusion) | data formatting | bytes 2146304 | tf_op jit(solution)/shard_map/concatenate | solution.py:62
  135.8 9.6 %all-to-all-start.2 = ((bf16[8,131,512]{2,1,0:T(8,128)(2,1)}), bf16[8,131,512]{2,1,0:T(8,128)(2,1)S(1)}, u32[]{:S(2)}, u32[]{:S(2)}) async-start(bf16[8,131,512]{2,1,0:T(8,128)(2,1)} %copy.126), calls=%async_computation.2 | async-start | bytes 2228224 | tf_op jit(solution)/shard_map/all_to_all | solution.py:65
  145.5 4.0 %fusion.18 = bf16[2,64,4,128]{3,1,2,0:T(8,128)(2,1)S(1)} fusion(f32[2,4,64,256]{3,2,1,0:T(8,128)} %fusion.28, bf16[2,256,4,128]{3,2,1,0:T(4,128)(2,1)S(1)} %copy-done.3, f32[2,4,64,256]{3,2,1,0:T(8,128)} %get-tuple-element.34, f32[2,4,64]{2,1,0:T(4,128)S(1)} %get-tuple-element.33), kind=kOutput, calls=%fused_computation.25 | convolution fusion | flops 34538240 | bytes 1705984 | tf_op jit(solution)/shard_map/chrk,ckhd->crhd/dot_general | solution.py:110
  149.7 4.1 %collective-permute-start.1 = (bf16[63,512]{1,0:T(8,128)(2,1)S(1)}, bf16[63,512]{1,0:T(8,128)(2,1)S(1)}, u32[]{:S(2)}, u32[]{:S(2)}) collective-permute-start(bf16[63,512]{1,0:T(8,128)(2,1)S(1)} %slice.51), channel_id=1, source_target_pairs={{0,8},{8,16},{16,24},{24,32},{32,40},{40,48},{48,56},{56,64},{64,7... | collective-permute-start | bytes 193544 | tf_op jit(solution)/shard_map/ppermute | solution.py:17
  153.8 2.2 %fusion.17 = bf16[2,64,4,128]{3,1,2,0:T(8,128)(2,1)S(1)} fusion(bf16[2,256,4,128]{3,2,1,0:T(4,128)(2,1)S(1)} %copy-done.1, f32[2,4,64]{2,1,0:T(4,128)S(1)} %get-tuple-element.33, f32[2,4,64,256]{3,2,1,0:T(8,128)} %copy-done.2), kind=kOutput, calls=%fused_computation.24 | convolution fusion | flops 34013952 | bytes 1181696 | tf_op jit(solution)/shard_map/chrk,ckhd->crhd/dot_general | solution.py:101
  163.1 18.2 %collective-permute-done.1 = bf16[63,512]{1,0:T(8,128)(2,1)S(1)} collective-permute-done((bf16[63,512]{1,0:T(8,128)(2,1)S(1)}, bf16[63,512]{1,0:T(8,128)(2,1)S(1)}, u32[]{:S(2)}, u32[]{:S(2)}) %collective-permute-start.1) | collective-permute-done | bytes 64544 | tf_op jit(solution)/shard_map/ppermute | solution.py:17
  184.3 1.9 %mul.93 = f32[8,128,512]{2,1,0:T(8,128)} reshape(f32[8,128,4,128]{3,2,1,0:T(4,128)S(1)} %mul.92) | data formatting | bytes 4194304 | tf_op jit(solution)/shard_map/mul | solution.py:75
  186.2 1.9 %multiply_reduce_fusion = f32[128,512]{1,0:T(8,128)S(1)} fusion(f32[8,128,512]{2,1,0:T(8,128)} %mul.93, bf16[8,131,512]{2,1,0:T(8,128)(2,1)S(1)} %all-to-all-done.2), kind=kLoop, calls=%fused_computation.13 | loop fusion | flops 1507328 | bytes 3407872 | tf_op jit(solution)/shard_map/reduce_sum | solution.py:75
  (67 shorter events, 22.0 us)
Async XLA Ops:
  0.6 13.2 %copy-start.5 = (bf16[128,512]{1,0:T(8,128)(2,1)S(1)}, bf16[128,512]{1,0:T(8,128)(2,1)}, u32[]{:S(2)}) copy-start(bf16[128,512]{1,0:T(8,128)(2,1)} %param.10) | copy-start | bytes 393220
  0.6 21.6 %copy-start.6 = (bf16[128,512]{1,0:T(8,128)(2,1)S(1)}, bf16[128,512]{1,0:T(8,128)(2,1)}, u32[]{:S(2)}) copy-start(bf16[128,512]{1,0:T(8,128)(2,1)} %param.7) | copy-start | bytes 393220
  0.7 21.8 %copy-start.4 = (bf16[512,512]{1,0:T(8,128)(2,1)S(1)}, bf16[512,512]{1,0:T(8,128)(2,1)}, u32[]{:S(2)}) copy-start(bf16[512,512]{1,0:T(8,128)(2,1)} %param.12) | copy-start | bytes 1572868
  1.9 21.4 %copy-start.7 = (bf16[128,512]{1,0:T(8,128)(2,1)S(1)}, bf16[128,512]{1,0:T(8,128)(2,1)}, u32[]{:S(2)}) copy-start(bf16[128,512]{1,0:T(8,128)(2,1)} %param.13) | copy-start | bytes 393220
  3.5 61.5 %all-to-all-start = ((bf16[8,128,1024]{1,2,0:T(8,128)(2,1)}), bf16[8,128,1024]{1,2,0:T(8,128)(2,1)S(1)}, u32[]{:S(2)}, u32[]{:S(2)}) async-start(bf16[8,128,1024]{1,2,0:T(8,128)(2,1)} %broadcast_in_dim.31), calls=%async_computation | async-start | bytes 4194304 | tf_op jit(solution)/shard_map/all_to_all | solution.py:22
  14.5 65.5 %collective-permute-start = (bf16[63,512]{1,0:T(8,128)(2,1)}, bf16[63,512]{1,0:T(8,128)(2,1)}, u32[]{:S(2)}, u32[]{:S(2)}) collective-permute-start(bf16[63,512]{1,0:T(8,128)(2,1)} %slice.41), channel_id=1, source_target_pairs={{8,0},{16,8},{24,16},{32,24},{40,32},{48,40},{56,48},{64,56},{72,6... | collective-permute-start | bytes 193544 | tf_op jit(solution)/shard_map/ppermute | solution.py:17
  66.2 33.2 %all-to-all-start.1 = ((bf16[8,128,512]{1,2,0:T(8,128)(2,1)}), bf16[8,128,512]{1,2,0:T(8,128)(2,1)}, u32[]{:S(2)}, u32[]{:S(2)}) async-start(bf16[8,128,512]{1,2,0:T(8,128)(2,1)} %broadcast_in_dim.33), calls=%async_computation.1 | async-start | bytes 2097152 | tf_op jit(solution)/shard_map/all_to_all | solution.py:22
  82.3 0.8 copy-start.2
  100.3 35.6 %all-to-all-start.3 = ((f32[512,1,1]{2,1,0:T(1,128)}), f32[512,1,1]{2,1,0:T(1,128)S(1)}, u32[]{:S(2)}, u32[]{:S(2)}) async-start(f32[512,1,1]{2,1,0:T(1,128)} %broadcast_in_dim.62), calls=%async_computation.3 | async-start | bytes 524288 | tf_op jit(solution)/shard_map/all_to_all | solution.py:124
  117.5 5.7 %copy-start = (f32[4,1024,8,128]{3,1,2,0:T(8,128)}, f32[4,1024,8,128]{3,1,2,0:T(8,128)S(1)}, u32[]{:S(2)}) copy-start(f32[4,1024,8,128]{3,1,2,0:T(8,128)S(1)} %get-tuple-element.32) | copy-start | bytes 50331652
  133.7 11.8 %copy-start.3 = (bf16[2,256,4,128]{3,2,1,0:T(4,128)(2,1)S(1)}, bf16[2,256,4,128]{3,2,1,0:T(4,128)(2,1)}, u32[]{:S(2)}) copy-start(bf16[2,256,4,128]{3,2,1,0:T(4,128)(2,1)} %reshape.114) | copy-start | bytes 1572868
  133.7 20.1 %copy-start.1 = (bf16[2,256,4,128]{3,2,1,0:T(4,128)(2,1)S(1)}, bf16[2,256,4,128]{3,2,1,0:T(4,128)(2,1)}, u32[]{:S(2)}) copy-start(bf16[2,256,4,128]{3,2,1,0:T(4,128)(2,1)} %reshape.115) | copy-start | bytes 1572868
  135.8 46.2 %all-to-all-start.2 = ((bf16[8,131,512]{2,1,0:T(8,128)(2,1)}), bf16[8,131,512]{2,1,0:T(8,128)(2,1)S(1)}, u32[]{:S(2)}, u32[]{:S(2)}) async-start(bf16[8,131,512]{2,1,0:T(8,128)(2,1)} %copy.126), calls=%async_computation.2 | async-start | bytes 2228224 | tf_op jit(solution)/shard_map/all_to_all | solution.py:65
  149.7 31.6 %collective-permute-start.1 = (bf16[63,512]{1,0:T(8,128)(2,1)S(1)}, bf16[63,512]{1,0:T(8,128)(2,1)S(1)}, u32[]{:S(2)}, u32[]{:S(2)}) collective-permute-start(bf16[63,512]{1,0:T(8,128)(2,1)S(1)} %slice.51), channel_id=1, source_target_pairs={{0,8},{8,16},{16,24},{24,32},{32,40},{40,48},{48,56},{56,64},{64,7... | collective-permute-start | bytes 193544 | tf_op jit(solution)/shard_map/ppermute | solution.py:17
